TPU v7x, 512 devices: a whole 4x4x16 slice. The times are simulated.
512 devices in a mesh: ctx: 64 (over z_hi, y, x), ch: 8 (over z_lo, core).
Axes of the slice: x: 4, y: 4, z: 16 (z_hi: 4, z_lo: 4; z = z_hi * 4 + z_lo), core: 2. Of those that a mesh axis runs over, the one named last changes fastest.
Arguments:
- first_gate: bfloat16 [8192, 8192], P('ctx', 'ch'), may hold values from -6 to 6
- second_gate: bfloat16 [8192, 8192], P('ctx', 'ch'), may hold values from -6 to 6
- output_gate: bfloat16 [8192, 8192], P('ctx', 'ch'), may hold values from -6 to 6
- values: bfloat16 [8192, 8192], P('ctx', 'ch'), may hold values from -6 to 6
- cotangent: bfloat16 [8192, 8192], P('ctx', 'ch'), may hold values from -6 to 6
- medium_filter: bfloat16 [128, 512], P(None, 'ch'), may hold values from -0.5 to 0.5
- long_filter: bfloat16 [8192, 512], P('ctx', 'ch'), may hold values from -0.044194174 to 0.044194174
Outputs:
- grad_first: bfloat16 [8192, 8192], P('ctx', 'ch')
- grad_second: bfloat16 [8192, 8192], P('ctx', 'ch')
- grad_output_gate: bfloat16 [8192, 8192], P('ctx', 'ch')
- grad_values: bfloat16 [8192, 8192], P('ctx', 'ch')
- grad_medium: float32 [128, 512], P(None, 'ch')
- grad_long: bfloat16 [8192, 512], P('ctx', 'ch')
- filter_rms: float32 [], replicated
All inputs are finite; a program needn't handle non-finite values.
Results may differ from a plain program's by a relative error of at most 0.011.
Values may be sent and summed in bfloat16 or wider, within the bound.
No kernel may reach another device: no remote copies, remote signals or barrier semaphores. Data moves between devices by JAX's collectives and lax.ppermute only.
A program may use at most 64 MiB of HBM per device.

v0:
```python
import math

import jax
import jax.numpy as jnp
from jax import lax
from jax.sharding import PartitionSpec as P

radix_cols = 128
block_limit = 64
highest = lax.Precision.HIGHEST
wide_type = jnp.float32
narrow_type = jnp.bfloat16


def passed_along(array, axis, by):
    peers = lax.axis_size(axis)
    pairs = [(i, i + by) for i in range(peers) if 0 <= i + by < peers]
    return lax.ppermute(array, axis, pairs)


def band_table(filt, block_rows, flipped):
    tap_count, group_count = filt.shape
    window_rows = block_rows + tap_count - 1
    leading = filt[::-1] if flipped else filt
    padded = jnp.concatenate([leading.T, jnp.zeros((group_count, block_rows), filt.dtype)], axis=1)
    tiled = jnp.broadcast_to(padded[:, None, :], (group_count, block_rows, window_rows + 1))
    tiled = tiled.reshape(group_count, block_rows * (window_rows + 1))
    return tiled[:, : block_rows * window_rows].reshape(group_count, block_rows, window_rows)


def windows_of(extended, block_rows, block_count, window_rows):
    return jnp.stack(
        [
            extended[number * block_rows : number * block_rows + window_rows]
            for number in range(block_count)
        ]
    )


def phase_table(row_count, col_count, period):
    row_ids = lax.broadcasted_iota(jnp.int32, (row_count, col_count), 0)
    col_ids = lax.broadcasted_iota(jnp.int32, (row_count, col_count), 1)
    angle = (row_ids * col_ids % period).astype(wide_type) * (2.0 * math.pi / period)
    return (jnp.cos(angle), jnp.sin(angle))


def forward_dft(signal, tables):
    outer_table, cos_twist, sin_twist, forward_inner, inverse_inner = tables
    outer = jnp.einsum("kna,nmb->mkab", outer_table, signal, precision=highest)
    real_part = outer[:, 0]
    imag_part = outer[:, 1]
    twisted = jnp.stack(
        [
            real_part * cos_twist + imag_part * sin_twist,
            imag_part * cos_twist - real_part * sin_twist,
        ],
        axis=1,
    )
    return jnp.einsum("mkab,kjbq->mjaq", twisted, forward_inner, precision=highest)


def inverse_dft(spectrum, tables, total_len):
    outer_table, cos_twist, sin_twist, forward_inner, inverse_inner = tables
    inner = jnp.einsum("mkab,kjbq->mjaq", spectrum, inverse_inner, precision=highest)
    real_part = inner[:, 0]
    imag_part = inner[:, 1]
    twisted = jnp.stack(
        [
            real_part * cos_twist - imag_part * sin_twist,
            imag_part * cos_twist + real_part * sin_twist,
        ],
        axis=1,
    )
    signal = jnp.einsum("kna,mkab->nmb", outer_table, twisted, precision=highest)
    return signal / total_len


def split_wide(value):
    high = value.astype(narrow_type)
    low = (value - high.astype(wide_type)).astype(narrow_type)
    return high, low


def joined_wide(high, low):
    return high.astype(wide_type) + low.astype(wide_type)


def butterfly_sum(value, axis):
    peers = lax.axis_size(axis)
    step = 1
    while step < peers:
        pairs = [(i, i ^ step) for i in range(peers)]
        value = value + lax.ppermute(value, axis, pairs)
        step *= 2
    return value


def medium_bands(filt):
    tap_count, item_count = filt.shape
    bands = band_table(filt, tap_count, False)
    near = bands[:, :, :tap_count]
    far = jnp.concatenate(
        [bands[:, :, tap_count:], jnp.zeros((item_count, tap_count, 1), filt.dtype)], axis=2
    )
    return near, far


def channel_work(pieces, filt):
    gated_part, grad_part, gate_part, filter_part = pieces
    half_rows = gated_part.shape[0]
    chan_total = gated_part.shape[1]
    item_count = filter_part.shape[1]
    group_size = chan_total // item_count
    seq_len = half_rows * radix_cols
    full_rows = 2 * half_rows
    total_len = 2 * seq_len
    scale = 1.0 / math.sqrt(seq_len * group_size)
    by_item = (half_rows, item_count, group_size, radix_cols)
    near, far = medium_bands(filt)

    gated_items = gated_part.reshape(by_item)
    gated_prev = jnp.concatenate([jnp.zeros_like(gated_items[:1]), gated_items[:-1]], axis=0)
    mixed = (
        jnp.einsum("ngcs,gsr->ngcr", gated_items, near, preferred_element_type=wide_type)
        + jnp.einsum("ngcs,gsr->ngcr", gated_prev, far, preferred_element_type=wide_type)
    ).reshape(half_rows, chan_total, radix_cols)
    gate_wide = gate_part.astype(wide_type)
    carried = (gate_wide * mixed).astype(narrow_type)

    cos_outer, sin_outer = phase_table(half_rows, full_rows, full_rows)
    cos_twist, sin_twist = phase_table(full_rows, radix_cols, total_len)
    cos_inner, sin_inner = phase_table(radix_cols, radix_cols, radix_cols)
    outer_table = jnp.stack([cos_outer, -sin_outer])
    forward_inner = jnp.stack(
        [jnp.stack([cos_inner, -sin_inner]), jnp.stack([sin_inner, cos_inner])]
    )
    inverse_inner = jnp.stack(
        [jnp.stack([cos_inner, sin_inner]), jnp.stack([-sin_inner, cos_inner])]
    )
    tables = (outer_table, cos_twist, sin_twist, forward_inner, inverse_inner)
    shaped = (item_count, group_size, 2, full_rows, radix_cols)
    flat_shape = (chan_total, 2, full_rows, radix_cols)
    signals = jnp.concatenate([carried, grad_part], axis=1).astype(wide_type)
    both_specs = forward_dft(signals, tables)
    gated_spec = both_specs[:chan_total].reshape(shaped)
    inner_spec = both_specs[chan_total:].reshape(shaped)
    filt_spec = forward_dft(filter_part.astype(wide_type), tables)[:, None]
    gated_re = gated_spec[:, :, 0]
    gated_im = gated_spec[:, :, 1]
    inner_re = inner_spec[:, :, 0]
    inner_im = inner_spec[:, :, 1]
    filt_re = filt_spec[:, :, 0]
    filt_im = filt_spec[:, :, 1]
    conv_spec = jnp.stack(
        [gated_re * filt_re - gated_im * filt_im, gated_re * filt_im + gated_im * filt_re], axis=2
    )
    back_spec = jnp.stack(
        [inner_re * filt_re + inner_im * filt_im, inner_im * filt_re - inner_re * filt_im], axis=2
    )
    corr_spec = jnp.stack(
        [inner_re * gated_re + inner_im * gated_im, inner_im * gated_re - inner_re * gated_im],
        axis=2,
    )
    signals_back = inverse_dft(
        jnp.concatenate([conv_spec.reshape(flat_shape), back_spec.reshape(flat_shape)], axis=0),
        tables,
        total_len,
    )
    second_mix = signals_back[:, :chan_total].astype(narrow_type)
    grad_carried = signals_back[:, chan_total:].astype(narrow_type).astype(wide_type)
    summed = jnp.sum(corr_spec, axis=1)
    lagged = (inverse_dft(summed, tables, total_len) * scale).astype(narrow_type)

    grad_second = (grad_carried * mixed).astype(narrow_type)
    grad_mixed = (grad_carried * gate_wide).astype(narrow_type)
    mixed_items = grad_mixed.reshape(by_item)
    mixed_next = jnp.concatenate([mixed_items[1:], jnp.zeros_like(mixed_items[:1])], axis=0)
    grad_gated = (
        jnp.einsum("ngcs,grs->ngcr", mixed_items, near, preferred_element_type=wide_type)
        + jnp.einsum("ngcs,grs->ngcr", mixed_next, far, preferred_element_type=wide_type)
    ).reshape(half_rows, chan_total, radix_cols)
    tap_count = filt.shape[0]
    own_lags = jnp.einsum(
        "ngcs,ngcr->gsr", gated_items, mixed_items, preferred_element_type=wide_type
    )
    prev_lags = jnp.einsum(
        "ngcs,ngcr->gsr", gated_prev, mixed_items, preferred_element_type=wide_type
    )
    lag_table = jnp.concatenate([own_lags, prev_lags], axis=2).reshape(item_count, -1)
    lag_table = jnp.concatenate(
        [lag_table, jnp.zeros((item_count, tap_count), wide_type)], axis=1
    ).reshape(item_count, tap_count, 2 * tap_count + 1)
    grad_medium = jnp.sum(lag_table[:, :, :tap_count], axis=1) * scale
    squares = jnp.sum(jnp.square(lagged.astype(wide_type))) + jnp.sum(grad_medium * grad_medium)
    squares = butterfly_sum(squares, "ch")
    medium_high, medium_low = split_wide(grad_medium)
    squares_high, squares_low = split_wide(squares)
    squares_row = jnp.zeros((1, radix_cols), narrow_type)
    squares_row = squares_row.at[0, 0].set(squares_high).at[0, 1].set(squares_low)
    shared = jnp.concatenate([medium_high, medium_low, squares_row], axis=0)
    shared = jnp.broadcast_to(shared[None], (half_rows,) + shared.shape)
    return jnp.concatenate(
        [second_mix, grad_second, grad_gated.astype(narrow_type), lagged, shared], axis=1
    )


def body(first_gate, second_gate, output_gate, values, cotangent, medium_filter, long_filter):
    tok_rows, chan_local = first_gate.shape
    tap_count, local_groups = medium_filter.shape
    group_size = chan_local // local_groups
    ctx_devices = lax.axis_size("ctx")
    ctx_groups = local_groups // ctx_devices
    chan_share = ctx_groups * group_size
    first_wide = first_gate.astype(wide_type)
    values_wide = values.astype(wide_type)
    cotangent_wide = cotangent.astype(wide_type)
    gated_input = (first_wide * values_wide).astype(narrow_type)
    grad_inner = (cotangent_wide * output_gate.astype(wide_type)).astype(narrow_type)

    def token_major(matrix):
        return matrix.T.reshape(ctx_devices, -1, tok_rows)

    outbound = jnp.concatenate(
        [
            token_major(gated_input),
            token_major(grad_inner),
            token_major(second_gate),
            token_major(long_filter),
        ],
        axis=1,
    )
    arrived = lax.all_to_all(outbound, "ctx", 0, 0, tiled=True)
    own_filter = lax.dynamic_slice_in_dim(
        medium_filter, lax.axis_index("ctx") * ctx_groups, ctx_groups, axis=1
    )
    returned = channel_work(
        (
            arrived[:, :chan_share],
            arrived[:, chan_share : 2 * chan_share],
            arrived[:, 2 * chan_share : 3 * chan_share],
            arrived[:, 3 * chan_share :],
        ),
        own_filter,
    )
    back = lax.all_to_all(returned, "ctx", 0, 0, tiled=True)

    def token_rows(start, count):
        return back[:, start : start + count].reshape(ctx_devices * count, tok_rows).T

    second_mix = token_rows(0, chan_share)
    grad_second = token_rows(chan_share, chan_share)
    grad_gated = token_rows(2 * chan_share, chan_share).astype(wide_type)
    grad_long = token_rows(3 * chan_share, ctx_groups)
    grad_medium = joined_wide(
        token_rows(3 * chan_share + ctx_groups, ctx_groups),
        token_rows(3 * chan_share + 2 * ctx_groups, ctx_groups),
    )
    squares_row = back[:, 3 * chan_share + 3 * ctx_groups]
    total_squares = jnp.sum(joined_wide(squares_row[:, 0], squares_row[:, 1]))
    grad_output_gate = (cotangent_wide * second_mix.astype(wide_type)).astype(narrow_type)
    grad_first = (grad_gated * values_wide).astype(narrow_type)
    grad_values = (grad_gated * first_wide).astype(narrow_type)
    entries = (tok_rows * ctx_devices + tap_count) * local_groups * lax.axis_size("ch")
    filter_rms = jnp.sqrt(total_squares / entries)
    return (
        grad_first,
        grad_second,
        grad_output_gate,
        grad_values,
        grad_medium,
        grad_long,
        filter_rms,
    )


def solution(mesh):
    return jax.shard_map(
        body,
        mesh=mesh,
        in_specs=(
            P("ctx", "ch"),
            P("ctx", "ch"),
            P("ctx", "ch"),
            P("ctx", "ch"),
            P("ctx", "ch"),
            P(None, "ch"),
            P("ctx", "ch"),
        ),
        out_specs=(
            P("ctx", "ch"),
            P("ctx", "ch"),
            P("ctx", "ch"),
            P("ctx", "ch"),
            P(None, "ch"),
            P("ctx", "ch"),
            P(),
        ),
        check_vma=False,
    )
```

profile of v0, /device:TPU:1, one launch (start us, length us, event | category | flops | bytes accessed | tf_op | source)
XLA Modules:
  0.0 198.8 jit_solution(3215432040798231159)
XLA Ops:
  0.7 1.2 copy.74
  1.8 1.1 copy.75
  3.0 1.1 copy.76
  4.1 1.1 copy.77
  5.6 1.0 pad_maximum_fusion
  6.6 21.7 %all-to-all-start = ((bf16[64,49,128]{2,1,0:T(8,128)(2,1)}), bf16[64,49,128]{2,1,0:T(8,128)(2,1)S(1)}, u32[]{:S(2)}, u32[]{:S(2)}) async-start(bf16[64,49,128]{2,1,0:T(8,128)(2,1)} %pad_maximum_fusion), calls=%async_computation | async-start | bytes 1835008 | tf_op jit(solution)/shard_map/all_to_all | solution.py:232
  32.8 37.3 %all-to-all-done = bf16[64,49,128]{2,1,0:T(8,128)(2,1)S(1)} async-done(((bf16[64,49,128]{2,1,0:T(8,128)(2,1)}), bf16[64,49,128]{2,1,0:T(8,128)(2,1)S(1)}, u32[]{:S(2)}, u32[]{:S(2)}) %all-to-all-start) | async-done | bytes 802848 | tf_op jit(solution)/shard_map/all_to_all | solution.py:232
  70.9 1.0 fusion.33
  71.9 1.8 convolution_bitcast_fusion
  74.6 3.8 %fusion.12 = f32[32,2,128,128]{2,3,0,1:T(8,128)S(1)} fusion(f32[32,1,128,128]{2,3,1,0:T(8,128)S(1)} %get-tuple-element.55, f32[32,1,128,128]{2,3,1,0:T(8,128)S(1)} %get-tuple-element.54, f32[1,2,128,128]{2,3,0,1:T(8,128)S(1)} %get-tuple-element.81, f32[1,2,128,128]{2,3,0,1:T(8,128)S(1)} %get-tuple-element.88), kind=kOutput, calls=%fused_computation.12 | convolution fusion | flops 3222339584 | bytes 8650752 | tf_op jit(solution)/shard_map/mkab,kjbq->mjaq/dot_general | solution.py:59
  81.0 4.0 %fusion.9 = f32[32,2,128,128]{2,3,1,0:T(8,128)S(1)} fusion(f32[16,2,128,128]{2,3,0,1:T(8,128)S(1)} %maximum_bitcast_fusion.6, f32[16,2,128,128]{2,3,0,1:T(8,128)S(1)} %maximum_bitcast_fusion.5, f32[1,2,128,128]{2,3,1,0:T(8,128)S(1)} %get-tuple-element.89, f32[1,2,128,128]{2,3,1,0:T(8,128)S(1)} %get-tuple-element.80), kind=kOutput, calls=%fused_computation.11 | convolution fusion | flops 3222339584 | bytes 8650752 | tf_op jit(solution)/shard_map/mkab,kjbq->mjaq/dot_general | solution.py:64
  85.9 4.1 %fusion.19 = bf16[64,32,128]{2,0,1:T(8,128)(2,1)S(1)} fusion(f32[32,1,128,128]{2,3,1,0:T(8,128)S(1)} %get-tuple-element.53, f32[32,1,128,128]{2,3,1,0:T(8,128)S(1)} %get-tuple-element.52, f32[1,64,128]{2,1,0:T(8,128)S(1)} %copy-done.7, f32[1,64,128]{2,1,0:T(8,128)S(1)} %copy-done.10), kind=kOutput, calls=%fused_computation.25 | convolution fusion | flops 806895616 | bytes 4784128 | tf_op jit(solution)/shard_map/kna,mkab->nmb/dot_general | solution.py:74
  90.7 1.0 fusion.96
  93.9 1.7 copy.93
  95.5 1.0 copy.128
  97.5 1.9 reshape.555
  100.5 1.1 bitcast_convert_fusion
  107.5 6.3 %collective-permute-start = (f32[]{:T(128)}, f32[]{:T(128)}, u32[]{:S(2)}, u32[]{:S(2)}) collective-permute-start(f32[]{:T(128)} %add.224), channel_id=1, source_target_pairs={{0,1},{1,0},{2,3},{3,2},{4,5},{5,4},{6,7},{7,6},{8,9},{9,8},{10,11... | collective-permute-start | bytes 20 | tf_op jit(solution)/shard_map/ppermute | solution.py:93
  114.4 10.5 %collective-permute-start.1 = (f32[]{:T(128)}, f32[]{:T(128)}, u32[]{:S(2)}, u32[]{:S(2)}) collective-permute-start(f32[]{:T(128)} %add.225), channel_id=1, source_target_pairs={{0,2},{1,3},{2,0},{3,1},{4,6},{5,7},{6,4},{7,5},{8,10},{9,11},{10,... | collective-permute-start | bytes 20 | tf_op jit(solution)/shard_map/ppermute | solution.py:93
  125.7 4.7 %collective-permute-start.2 = (f32[]{:T(128)}, f32[]{:T(128)}, u32[]{:S(2)}, u32[]{:S(2)}) collective-permute-start(f32[]{:T(128)} %add.226), channel_id=1, source_target_pairs={{0,4},{1,5},{2,6},{3,7},{4,0},{5,1},{6,2},{7,3},{8,12},{9,13},{10,... | collective-permute-start | bytes 20 | tf_op jit(solution)/shard_map/ppermute | solution.py:93
  132.2 1.8 fusion.114
  134.0 1.3 scatter.9
  135.9 1.7 copy.94
  137.7 53.6 %all_to_all.10 = bf16[64,52,128]{2,1,0:T(8,128)(2,1)S(1)} all-to-all(bf16[64,52,128]{2,1,0:T(8,128)(2,1)S(1)} %copy.94), channel_id=1, replica_groups=mesh['ctx'=64,'ch'=8] {'ctx'}, dimensions={0} | all-to-all | bytes 1703936 | tf_op jit(solution)/shard_map/all_to_all | solution.py:245
  (110 shorter events, 26.0 us)
Async XLA Ops:
  0.6 27.7 %copy-start = (bf16[128,64]{0,1:T(8,128)(2,1)S(1)}, bf16[128,64]{0,1:T(8,128)(2,1)}, u32[]{:S(2)}) copy-start(bf16[128,64]{0,1:T(8,128)(2,1)} %param.16) | copy-start | bytes 49156
  0.6 4.6 %copy-start.16 = (bf16[128,1024]{1,0:T(8,128)(2,1)S(1)}, bf16[128,1024]{1,0:T(8,128)(2,1)}, u32[]{:S(2)}) copy-start(bf16[128,1024]{1,0:T(8,128)(2,1)} %param.12) | copy-start | bytes 786436
  0.7 4.7 %copy-start.17 = (bf16[128,64]{0,1:T(8,128)(2,1)S(1)}, bf16[128,64]{0,1:T(8,128)(2,1)}, u32[]{:S(2)}) copy-start(bf16[128,64]{0,1:T(8,128)(2,1)} %param.17) | copy-start | bytes 49156
  6.6 63.5 %all-to-all-start = ((bf16[64,49,128]{2,1,0:T(8,128)(2,1)}), bf16[64,49,128]{2,1,0:T(8,128)(2,1)S(1)}, u32[]{:S(2)}, u32[]{:S(2)}) async-start(bf16[64,49,128]{2,1,0:T(8,128)(2,1)} %pad_maximum_fusion), calls=%async_computation | async-start | bytes 1835008 | tf_op jit(solution)/shard_map/all_to_all | solution.py:232
  29.2 41.4 %copy-start.12 = (bf16[1,128,255]{2,1,0:T(8,128)(2,1)}, bf16[1,128,255]{2,1,0:T(8,128)(2,1)S(1)}, u32[]{:S(2)}) copy-start(bf16[1,128,255]{2,1,0:T(8,128)(2,1)S(1)} %reshape.541) | copy-start | bytes 195844
  31.9 46.8 %copy-start.6 = (f32[1,64,128]{2,1,0:T(8,128)}, f32[1,64,128]{2,1,0:T(8,128)S(1)}, u32[]{:S(2)}) copy-start(f32[1,64,128]{2,1,0:T(8,128)S(1)} %get-tuple-element.96) | copy-start | bytes 98308
  31.9 46.8 %copy-start.9 = (f32[1,64,128]{2,1,0:T(8,128)}, f32[1,64,128]{2,1,0:T(8,128)S(1)}, u32[]{:S(2)}) copy-start(f32[1,64,128]{2,1,0:T(8,128)S(1)} %get-tuple-element.97) | copy-start | bytes 98308
  32.8 48.2 %copy-start.3 = (f32[1,2,128,128]{2,3,1,0:T(8,128)}, f32[1,2,128,128]{2,3,1,0:T(8,128)S(1)}, u32[]{:S(2)}) copy-start(f32[1,2,128,128]{2,3,1,0:T(8,128)S(1)} %get-tuple-element.89) | copy-start | bytes 393220
  70.1 0.8 copy-start.14
  85.0 0.9 copy-start.7
  85.0 0.9 copy-start.10
  85.9 4.8 %copy-start.13 = (bf16[1,128,255]{2,1,0:T(8,128)(2,1)S(1)}, bf16[1,128,255]{2,1,0:T(8,128)(2,1)}, u32[]{:S(2)}) copy-start(bf16[1,128,255]{2,1,0:T(8,128)(2,1)} %copy-done.12) | copy-start | bytes 195844
  99.5 2.8 %copy-start.4 = (f32[1,2,128,128]{2,3,1,0:T(8,128)S(1)}, f32[1,2,128,128]{2,3,1,0:T(8,128)}, u32[]{:S(2)}) copy-start(f32[1,2,128,128]{2,3,1,0:T(8,128)} %copy-done.3) | copy-start | bytes 393220
  99.5 3.5 %copy-start.1 = (f32[64,16,128]{2,0,1:T(8,128)S(1)}, f32[64,16,128]{2,0,1:T(8,128)}, u32[]{:S(2)}) copy-start(f32[64,16,128]{2,0,1:T(8,128)} %get-tuple-element.93) | copy-start | bytes 1572868
  99.5 4.3 %copy-start.2 = (f32[128,64,16]{0,1,2:T(8,128)S(1)}, f32[128,64,16]{0,1,2:T(8,128)}, u32[]{:S(2)}) copy-start(f32[128,64,16]{0,1,2:T(8,128)} %fusion.96) | copy-start | bytes 1572868
  99.5 4.3 %copy-start.5 = (bf16[63,1,16,128]{3,0,2,1:T(8,128)(2,1)S(1)}, bf16[63,1,16,128]{3,0,2,1:T(8,128)(2,1)}, u32[]{:S(2)}) copy-start(bf16[63,1,16,128]{3,0,2,1:T(8,128)(2,1)} %slice_bitcast_fusion.2) | copy-start | bytes 774148
  99.5 4.3 %copy-start.15 = (bf16[1,128,127]{2,1,0:T(8,128)(2,1)S(1)}, bf16[1,128,127]{2,1,0:T(8,128)(2,1)}, u32[]{:S(2)}) copy-start(bf16[1,128,127]{2,1,0:T(8,128)(2,1)} %slice.199) | copy-start | bytes 97540
  102.2 2.6 %copy-start.8 = (f32[1,64,128]{2,1,0:T(8,128)S(1)}, f32[1,64,128]{2,1,0:T(8,128)}, u32[]{:S(2)}) copy-start(f32[1,64,128]{2,1,0:T(8,128)} %copy-done.6) | copy-start | bytes 98308
  102.2 2.6 %copy-start.11 = (f32[1,64,128]{2,1,0:T(8,128)S(1)}, f32[1,64,128]{2,1,0:T(8,128)}, u32[]{:S(2)}) copy-start(f32[1,64,128]{2,1,0:T(8,128)} %copy-done.9) | copy-start | bytes 98308
  102.3 33.0 %copy-start.18 = (bf16[1,128]{1,0:T(2,128)(2,1)S(1)}, bf16[1,128]{1,0:T(2,128)(2,1)}, u32[]{:S(2)}) copy-start(bf16[1,128]{1,0:T(2,128)(2,1)} %get-tuple-element.90) | copy-start | bytes 772
  102.3 33.0 %copy-start.19 = (bf16[1,128]{1,0:T(2,128)(2,1)S(1)}, bf16[1,128]{1,0:T(2,128)(2,1)}, u32[]{:S(2)}) copy-start(bf16[1,128]{1,0:T(2,128)(2,1)} %fusion.100) | copy-start | bytes 772
  107.5 6.3 %collective-permute-start = (f32[]{:T(128)}, f32[]{:T(128)}, u32[]{:S(2)}, u32[]{:S(2)}) collective-permute-start(f32[]{:T(128)} %add.224), channel_id=1, source_target_pairs={{0,1},{1,0},{2,3},{3,2},{4,5},{5,4},{6,7},{7,6},{8,9},{9,8},{10,11... | collective-permute-start | bytes 20 | tf_op jit(solution)/shard_map/ppermute | solution.py:93
  114.4 10.6 %collective-permute-start.1 = (f32[]{:T(128)}, f32[]{:T(128)}, u32[]{:S(2)}, u32[]{:S(2)}) collective-permute-start(f32[]{:T(128)} %add.225), channel_id=1, source_target_pairs={{0,2},{1,3},{2,0},{3,1},{4,6},{5,7},{6,4},{7,5},{8,10},{9,11},{10,... | collective-permute-start | bytes 20 | tf_op jit(solution)/shard_map/ppermute | solution.py:93
  125.7 5.1 %collective-permute-start.2 = (f32[]{:T(128)}, f32[]{:T(128)}, u32[]{:S(2)}, u32[]{:S(2)}) collective-permute-start(f32[]{:T(128)} %add.226), channel_id=1, source_target_pairs={{0,4},{1,5},{2,6},{3,7},{4,0},{5,1},{6,2},{7,3},{8,12},{9,13},{10,... | collective-permute-start | bytes 20 | tf_op jit(solution)/shard_map/ppermute | solution.py:93
where the time goes:
time: 200 us; the launch traced here: 199 us
  blocking collectives  53.6 us (27%)
  starting transfers between devices  43.3 us (22%)
  waiting for transfers between devices  37.9 us (19%)
  local copies, waits for them, and re-layouts  22.6 us (11%)
  matrix products  19.4 us (10%)
  other arithmetic  15.3 us (8%)
  between operations  6.89 us (3%)
    all_to_all x1, blocking collectives, body(): back = lax.all_to_all(returned, 'ctx', 0, 0, tiled=True)  53.6 us
    all_to_all x1, waiting for transfers between devices, body(): arrived = lax.all_to_all(outbound, 'ctx', 0, 0, tiled=True)  37.3 us
    all_to_all x1, starting transfers between devices, body(): arrived = lax.all_to_all(outbound, 'ctx', 0, 0, tiled=True)  21.7 us
    ppermute x3, starting transfers between devices, butterfly_sum(): value = value + lax.ppermute(value, axis, pairs)  21.5 us
    unnamed x57, local copies, waits for them, and re-layouts  11 us
    dot_general x2, matrix products, inverse_dft(): jnp.einsum('kna,mkab->nmb', outer_table, twisted, precision=highest)  4.95 us
    dot_general x2, matrix products, inverse_dft(): jnp.einsum('mkab,kjbq->mjaq', spectrum, inverse_inner, precision=highest)  4.4 us
    dot_general x2, matrix products, forward_dft(): jnp.einsum('mkab,kjbq->mjaq', twisted, forward_inner, precision=highest)  4.15 us
  transfers between devices with their start and end apart: 4, of which 3 were waited for; matrix products, arithmetic and copies ran while one was open for 2% of the time, Pallas kernels for 0%

commit v1 on v0

--- a/solution.py
+++ b/solution.py
@@ -85,14 +85,16 @@
     return high.astype(wide_type) + low.astype(wide_type)
 
 
-def butterfly_sum(value, axis):
+def gathered_sum(value, axis):
     peers = lax.axis_size(axis)
-    step = 1
-    while step < peers:
-        pairs = [(i, i ^ step) for i in range(peers)]
-        value = value + lax.ppermute(value, axis, pairs)
-        step *= 2
-    return value
+    source = lax.axis_index(axis)
+    slot_ids = lax.iota(jnp.int32, peers)
+    slots = jnp.where(slot_ids == source, value, 0.0)
+    for shift in range(1, peers):
+        pairs = [(i, (i + shift) % peers) for i in range(peers)]
+        got = lax.ppermute(value, axis, pairs)
+        slots = slots + jnp.where(slot_ids == (source - shift) % peers, got, 0.0)
+    return jnp.sum(slots)
 
 
 def medium_bands(filt):
@@ -192,11 +194,17 @@
     ).reshape(item_count, tap_count, 2 * tap_count + 1)
     grad_medium = jnp.sum(lag_table[:, :, :tap_count], axis=1) * scale
     squares = jnp.sum(jnp.square(lagged.astype(wide_type))) + jnp.sum(grad_medium * grad_medium)
-    squares = butterfly_sum(squares, "ch")
+    squares = gathered_sum(squares, "ch")
     medium_high, medium_low = split_wide(grad_medium)
     squares_high, squares_low = split_wide(squares)
-    squares_row = jnp.zeros((1, radix_cols), narrow_type)
-    squares_row = squares_row.at[0, 0].set(squares_high).at[0, 1].set(squares_low)
+    squares_row = jnp.concatenate(
+        [
+            squares_high.reshape(1, 1),
+            squares_low.reshape(1, 1),
+            jnp.zeros((1, radix_cols - 2), narrow_type),
+        ],
+        axis=1,
+    )
     shared = jnp.concatenate([medium_high, medium_low, squares_row], axis=0)
     shared = jnp.broadcast_to(shared[None], (half_rows,) + shared.shape)
     return jnp.concatenate(

time: 200 us -> 216 us (1.080)
  starting transfers between devices: 43.3 us -> 59.5 us
    ppermute x3 -> x7, starting transfers between devices: 21.5 us -> 37.7 us  [gathered_sum(): got = lax.ppermute(value, axis, pairs)]
    reduce_sum x0 -> x1, other arithmetic: none -> 4.98 us  [gathered_sum(): return jnp.sum(slots)]
    another operation x3 -> x0, other arithmetic: 3.17 us -> none
    unnamed x57 -> x59, local copies, waits for them, and re-layouts: 11 us -> 11 us
  transfers between devices with their start and end apart: 4 -> 8, of which waited for: 3 -> 2; matrix products, arithmetic and copies ran while one was open for 2% -> 1% of each run, Pallas kernels for 0% -> 0%
where the time goes in v1:
time: 216 us; the launch traced here: 215 us
  starting transfers between devices  59.5 us (28%)
  blocking collectives  53.8 us (25%)
  waiting for transfers between devices  39.6 us (18%)
  local copies, waits for them, and re-layouts  20.7 us (10%)
  matrix products  19.3 us (9%)
  other arithmetic  16.6 us (8%)
  between operations  5.72 us (3%)
    all_to_all x1, blocking collectives, body(): back = lax.all_to_all(returned, 'ctx', 0, 0, tiled=True)  53.8 us
    all_to_all x1, waiting for transfers between devices, body(): arrived = lax.all_to_all(outbound, 'ctx', 0, 0, tiled=True)  39.1 us
    ppermute x7, starting transfers between devices, gathered_sum(): got = lax.ppermute(value, axis, pairs)  37.7 us
    all_to_all x1, starting transfers between devices, body(): arrived = lax.all_to_all(outbound, 'ctx', 0, 0, tiled=True)  21.7 us
    unnamed x59, local copies, waits for them, and re-layouts  11 us
    reduce_sum x1, other arithmetic, gathered_sum(): return jnp.sum(slots)  4.98 us
    dot_general x2, matrix products, inverse_dft(): jnp.einsum('kna,mkab->nmb', outer_table, twisted, precision=highest)  4.95 us
    dot_general x2, matrix products, inverse_dft(): jnp.einsum('mkab,kjbq->mjaq', spectrum, inverse_inner, precision=highest)  4.35 us
  transfers between devices with their start and end apart: 8, of which 2 were waited for; matrix products, arithmetic and copies ran while one was open for 1% of the time, Pallas kernels for 0%

profile of v1, /device:TPU:1, one launch (start us, length us, event | category | flops | bytes accessed | tf_op | source)
XLA Modules:
  0.0 215.2 jit_solution(7891600108455643573)
XLA Ops:
  0.7 1.2 copy.74
  1.8 1.1 copy.75
  3.0 1.1 copy.76
  4.1 1.1 copy.77
  6.6 21.7 %all-to-all-start = ((bf16[64,49,128]{2,1,0:T(8,128)(2,1)}), bf16[64,49,128]{2,1,0:T(8,128)(2,1)S(1)}, u32[]{:S(2)}, u32[]{:S(2)}) async-start(bf16[64,49,128]{2,1,0:T(8,128)(2,1)} %pad_maximum_fusion), calls=%async_computation | async-start | bytes 1835008 | tf_op jit(solution)/shard_map/all_to_all | solution.py:240
  31.0 39.1 %all-to-all-done = bf16[64,49,128]{2,1,0:T(8,128)(2,1)S(1)} async-done(((bf16[64,49,128]{2,1,0:T(8,128)(2,1)}), bf16[64,49,128]{2,1,0:T(8,128)(2,1)S(1)}, u32[]{:S(2)}, u32[]{:S(2)}) %all-to-all-start) | async-done | bytes 802848 | tf_op jit(solution)/shard_map/all_to_all | solution.py:240
  71.9 1.8 convolution_bitcast_fusion
  74.6 3.8 %fusion.12 = f32[32,2,128,128]{2,3,0,1:T(8,128)S(1)} fusion(f32[32,1,128,128]{2,3,1,0:T(8,128)S(1)} %get-tuple-element.31, f32[32,1,128,128]{2,3,1,0:T(8,128)S(1)} %get-tuple-element.30, f32[1,2,128,128]{2,3,0,1:T(8,128)S(1)} %get-tuple-element.57, f32[1,2,128,128]{2,3,0,1:T(8,128)S(1)} %get-tuple-element.64), kind=kOutput, calls=%fused_computation.12 | convolution fusion | flops 3222339584 | bytes 8650752 | tf_op jit(solution)/shard_map/mkab,kjbq->mjaq/dot_general | solution.py:59
  81.0 4.0 %fusion.9 = f32[32,2,128,128]{2,3,1,0:T(8,128)S(1)} fusion(f32[16,2,128,128]{2,3,0,1:T(8,128)S(1)} %maximum_bitcast_fusion.6, f32[16,2,128,128]{2,3,0,1:T(8,128)S(1)} %maximum_bitcast_fusion.5, f32[1,2,128,128]{2,3,1,0:T(8,128)S(1)} %get-tuple-element.65, f32[1,2,128,128]{2,3,1,0:T(8,128)S(1)} %get-tuple-element.56), kind=kOutput, calls=%fused_computation.11 | convolution fusion | flops 3222339584 | bytes 8650752 | tf_op jit(solution)/shard_map/mkab,kjbq->mjaq/dot_general | solution.py:64
  85.9 4.1 %fusion.19 = bf16[64,32,128]{2,0,1:T(8,128)(2,1)S(1)} fusion(f32[32,1,128,128]{2,3,1,0:T(8,128)S(1)} %get-tuple-element.29, f32[32,1,128,128]{2,3,1,0:T(8,128)S(1)} %get-tuple-element.28, f32[1,64,128]{2,1,0:T(8,128)S(1)} %copy-done.7, f32[1,64,128]{2,1,0:T(8,128)S(1)} %copy-done.10), kind=kOutput, calls=%fused_computation.25 | convolution fusion | flops 806895616 | bytes 4784128 | tf_op jit(solution)/shard_map/kna,mkab->nmb/dot_general | solution.py:74
  90.6 1.1 fusion.96
  93.8 1.7 copy.93
  97.5 1.9 reshape.497
  100.4 1.1 bitcast_convert_fusion
  106.9 13.8 %collective-permute-start = (f32[]{:T(128)}, f32[]{:T(128)}, u32[]{:S(2)}, u32[]{:S(2)}) collective-permute-start(f32[]{:T(128)} %add.259), channel_id=1, source_target_pairs={{0,1},{1,2},{2,3},{3,4},{4,5},{5,6},{6,7},{7,0},{8,9},{9,10},{10,1... | collective-permute-start | bytes 20 | tf_op jit(solution)/shard_map/ppermute | solution.py:95
  120.7 3.6 %collective-permute-start.1 = (f32[]{:T(128)}, f32[]{:T(128)}, u32[]{:S(2)}, u32[]{:S(2)}) collective-permute-start(f32[]{:T(128)} %add.259), channel_id=1, source_target_pairs={{0,2},{1,3},{2,4},{3,5},{4,6},{5,7},{6,0},{7,1},{8,10},{9,11},{10,... | collective-permute-start | bytes 20 | tf_op jit(solution)/shard_map/ppermute | solution.py:95
  124.3 3.0 %collective-permute-start.2 = (f32[]{:T(128)}, f32[]{:T(128)}, u32[]{:S(2)}, u32[]{:S(2)}) collective-permute-start(f32[]{:T(128)} %add.259), channel_id=1, source_target_pairs={{0,3},{1,4},{2,5},{3,6},{4,7},{5,0},{6,1},{7,2},{8,11},{9,12},{10,... | collective-permute-start | bytes 20 | tf_op jit(solution)/shard_map/ppermute | solution.py:95
  127.3 4.6 %collective-permute-start.3 = (f32[]{:T(128)}, f32[]{:T(128)}, u32[]{:S(2)}, u32[]{:S(2)}) collective-permute-start(f32[]{:T(128)} %add.259), channel_id=1, source_target_pairs={{0,4},{1,5},{2,6},{3,7},{4,0},{5,1},{6,2},{7,3},{8,12},{9,13},{10,... | collective-permute-start | bytes 20 | tf_op jit(solution)/shard_map/ppermute | solution.py:95
  131.8 4.9 %collective-permute-start.4 = (f32[]{:T(128)}, f32[]{:T(128)}, u32[]{:S(2)}, u32[]{:S(2)}) collective-permute-start(f32[]{:T(128)} %add.259), channel_id=1, source_target_pairs={{0,5},{1,6},{2,7},{3,0},{4,1},{5,2},{6,3},{7,4},{8,13},{9,14},{10,... | collective-permute-start | bytes 20 | tf_op jit(solution)/shard_map/ppermute | solution.py:95
  136.8 3.2 %collective-permute-start.5 = (f32[]{:T(128)}, f32[]{:T(128)}, u32[]{:S(2)}, u32[]{:S(2)}) collective-permute-start(f32[]{:T(128)} %add.259), channel_id=1, source_target_pairs={{0,6},{1,7},{2,0},{3,1},{4,2},{5,3},{6,4},{7,5},{8,14},{9,15},{10,... | collective-permute-start | bytes 20 | tf_op jit(solution)/shard_map/ppermute | solution.py:95
  140.0 4.7 %collective-permute-start.6 = (f32[]{:T(128)}, f32[]{:T(128)}, u32[]{:S(2)}, u32[]{:S(2)}) collective-permute-start(f32[]{:T(128)} %add.259), channel_id=1, source_target_pairs={{0,7},{1,0},{2,1},{3,2},{4,3},{5,4},{6,5},{7,6},{8,15},{9,8},{10,9... | collective-permute-start | bytes 20 | tf_op jit(solution)/shard_map/ppermute | solution.py:95
  145.1 5.0 %fusion.108 = f32[]{:T(128)} fusion(f32[]{:T(128)} %collective-permute-done.6, s32[]{:T(128)S(6)} %select_n.189, f32[]{:T(128)} %collective-permute-done.5, s32[]{:T(128)S(6)} %select_n.187, f32[]{:T(128)} %collective-permute-done.4, s32[]{:T(128)S(6)} %select_n.185, f32[]{:T(128)} %collective-permute-done.3, s32[]{:T(128)S(6)} %select_n.183, ...), kind=kLoop, calls=%fused_computation.196 | loop fusion | flops 191 | bytes 68 | tf_op jit(solution)/shard_map/reduce_sum | solution.py:97
  152.1 1.7 copy.94
  153.9 53.8 %all_to_all.10 = bf16[64,52,128]{2,1,0:T(8,128)(2,1)S(1)} all-to-all(bf16[64,52,128]{2,1,0:T(8,128)(2,1)S(1)} %copy.94), channel_id=1, replica_groups=mesh['ctx'=64,'ch'=8] {'ctx'}, dimensions={0} | all-to-all | bytes 1703936 | tf_op jit(solution)/shard_map/all_to_all | solution.py:253
  (115 shorter events, 26.5 us)
Async XLA Ops:
  0.6 27.8 %copy-start = (bf16[128,64]{0,1:T(8,128)(2,1)S(1)}, bf16[128,64]{0,1:T(8,128)(2,1)}, u32[]{:S(2)}) copy-start(bf16[128,64]{0,1:T(8,128)(2,1)} %param.12) | copy-start | bytes 49156
  0.6 4.6 %copy-start.16 = (bf16[128,1024]{1,0:T(8,128)(2,1)S(1)}, bf16[128,1024]{1,0:T(8,128)(2,1)}, u32[]{:S(2)}) copy-start(bf16[128,1024]{1,0:T(8,128)(2,1)} %param.8) | copy-start | bytes 786436
  0.7 4.7 %copy-start.17 = (bf16[128,64]{0,1:T(8,128)(2,1)S(1)}, bf16[128,64]{0,1:T(8,128)(2,1)}, u32[]{:S(2)}) copy-start(bf16[128,64]{0,1:T(8,128)(2,1)} %param.13) | copy-start | bytes 49156
  6.6 63.5 %all-to-all-start = ((bf16[64,49,128]{2,1,0:T(8,128)(2,1)}), bf16[64,49,128]{2,1,0:T(8,128)(2,1)S(1)}, u32[]{:S(2)}, u32[]{:S(2)}) async-start(bf16[64,49,128]{2,1,0:T(8,128)(2,1)} %pad_maximum_fusion), calls=%async_computation | async-start | bytes 1835008 | tf_op jit(solution)/shard_map/all_to_all | solution.py:240
  29.3 41.3 %copy-start.12 = (bf16[1,128,255]{2,1,0:T(8,128)(2,1)}, bf16[1,128,255]{2,1,0:T(8,128)(2,1)S(1)}, u32[]{:S(2)}) copy-start(bf16[1,128,255]{2,1,0:T(8,128)(2,1)S(1)} %reshape.483) | copy-start | bytes 195844
  30.1 48.6 %copy-start.6 = (f32[1,64,128]{2,1,0:T(8,128)}, f32[1,64,128]{2,1,0:T(8,128)S(1)}, u32[]{:S(2)}) copy-start(f32[1,64,128]{2,1,0:T(8,128)S(1)} %get-tuple-element.72) | copy-start | bytes 98308
  30.1 48.6 %copy-start.9 = (f32[1,64,128]{2,1,0:T(8,128)}, f32[1,64,128]{2,1,0:T(8,128)S(1)}, u32[]{:S(2)}) copy-start(f32[1,64,128]{2,1,0:T(8,128)S(1)} %get-tuple-element.73) | copy-start | bytes 98308
  31.0 50.0 %copy-start.3 = (f32[1,2,128,128]{2,3,1,0:T(8,128)}, f32[1,2,128,128]{2,3,1,0:T(8,128)S(1)}, u32[]{:S(2)}) copy-start(f32[1,2,128,128]{2,3,1,0:T(8,128)S(1)} %get-tuple-element.65) | copy-start | bytes 393220
  85.9 4.8 %copy-start.13 = (bf16[1,128,255]{2,1,0:T(8,128)(2,1)S(1)}, bf16[1,128,255]{2,1,0:T(8,128)(2,1)}, u32[]{:S(2)}) copy-start(bf16[1,128,255]{2,1,0:T(8,128)(2,1)} %copy-done.12) | copy-start | bytes 195844
  99.4 2.9 %copy-start.1 = (f32[64,16,128]{2,0,1:T(8,128)S(1)}, f32[64,16,128]{2,0,1:T(8,128)}, u32[]{:S(2)}) copy-start(f32[64,16,128]{2,0,1:T(8,128)} %get-tuple-element.69) | copy-start | bytes 1572868
  99.4 3.7 %copy-start.2 = (f32[128,64,16]{0,1,2:T(8,128)S(1)}, f32[128,64,16]{0,1,2:T(8,128)}, u32[]{:S(2)}) copy-start(f32[128,64,16]{0,1,2:T(8,128)} %fusion.96) | copy-start | bytes 1572868
  99.4 3.7 %copy-start.5 = (bf16[63,1,16,128]{3,0,2,1:T(8,128)(2,1)S(1)}, bf16[63,1,16,128]{3,0,2,1:T(8,128)(2,1)}, u32[]{:S(2)}) copy-start(bf16[63,1,16,128]{3,0,2,1:T(8,128)(2,1)} %slice_bitcast_fusion.2) | copy-start | bytes 774148
  99.5 3.7 %copy-start.15 = (bf16[1,128,127]{2,1,0:T(8,128)(2,1)S(1)}, bf16[1,128,127]{2,1,0:T(8,128)(2,1)}, u32[]{:S(2)}) copy-start(bf16[1,128,127]{2,1,0:T(8,128)(2,1)} %slice.163) | copy-start | bytes 97540
  101.6 2.5 %copy-start.8 = (f32[1,64,128]{2,1,0:T(8,128)S(1)}, f32[1,64,128]{2,1,0:T(8,128)}, u32[]{:S(2)}) copy-start(f32[1,64,128]{2,1,0:T(8,128)} %copy-done.6) | copy-start | bytes 98308
  101.6 2.5 %copy-start.11 = (f32[1,64,128]{2,1,0:T(8,128)S(1)}, f32[1,64,128]{2,1,0:T(8,128)}, u32[]{:S(2)}) copy-start(f32[1,64,128]{2,1,0:T(8,128)} %copy-done.9) | copy-start | bytes 98308
  101.7 35.1 %copy-start.19 = (f32[128]{0:T(128)S(1)}, f32[128]{0:T(128)}, u32[]{:S(2)}) copy-start(f32[128]{0:T(128)} %copy-done.18) | copy-start | bytes 1540
  101.7 49.7 %copy-start.20 = (bf16[1,128]{1,0:T(2,128)(2,1)S(1)}, bf16[1,128]{1,0:T(2,128)(2,1)}, u32[]{:S(2)}) copy-start(bf16[1,128]{1,0:T(2,128)(2,1)} %get-tuple-element.66) | copy-start | bytes 772
  106.9 29.9 %collective-permute-start = (f32[]{:T(128)}, f32[]{:T(128)}, u32[]{:S(2)}, u32[]{:S(2)}) collective-permute-start(f32[]{:T(128)} %add.259), channel_id=1, source_target_pairs={{0,1},{1,2},{2,3},{3,4},{4,5},{5,6},{6,7},{7,0},{8,9},{9,10},{10,1... | collective-permute-start | bytes 20 | tf_op jit(solution)/shard_map/ppermute | solution.py:95
  120.7 19.3 %collective-permute-start.1 = (f32[]{:T(128)}, f32[]{:T(128)}, u32[]{:S(2)}, u32[]{:S(2)}) collective-permute-start(f32[]{:T(128)} %add.259), channel_id=1, source_target_pairs={{0,2},{1,3},{2,4},{3,5},{4,6},{5,7},{6,0},{7,1},{8,10},{9,11},{10,... | collective-permute-start | bytes 20 | tf_op jit(solution)/shard_map/ppermute | solution.py:95
  124.3 20.4 %collective-permute-start.2 = (f32[]{:T(128)}, f32[]{:T(128)}, u32[]{:S(2)}, u32[]{:S(2)}) collective-permute-start(f32[]{:T(128)} %add.259), channel_id=1, source_target_pairs={{0,3},{1,4},{2,5},{3,6},{4,7},{5,0},{6,1},{7,2},{8,11},{9,12},{10,... | collective-permute-start | bytes 20 | tf_op jit(solution)/shard_map/ppermute | solution.py:95
  127.3 17.4 %collective-permute-start.3 = (f32[]{:T(128)}, f32[]{:T(128)}, u32[]{:S(2)}, u32[]{:S(2)}) collective-permute-start(f32[]{:T(128)} %add.259), channel_id=1, source_target_pairs={{0,4},{1,5},{2,6},{3,7},{4,0},{5,1},{6,2},{7,3},{8,12},{9,13},{10,... | collective-permute-start | bytes 20 | tf_op jit(solution)/shard_map/ppermute | solution.py:95
  131.8 12.8 %collective-permute-start.4 = (f32[]{:T(128)}, f32[]{:T(128)}, u32[]{:S(2)}, u32[]{:S(2)}) collective-permute-start(f32[]{:T(128)} %add.259), channel_id=1, source_target_pairs={{0,5},{1,6},{2,7},{3,0},{4,1},{5,2},{6,3},{7,4},{8,13},{9,14},{10,... | collective-permute-start | bytes 20 | tf_op jit(solution)/shard_map/ppermute | solution.py:95
  136.8 7.9 %collective-permute-start.5 = (f32[]{:T(128)}, f32[]{:T(128)}, u32[]{:S(2)}, u32[]{:S(2)}) collective-permute-start(f32[]{:T(128)} %add.259), channel_id=1, source_target_pairs={{0,6},{1,7},{2,0},{3,1},{4,2},{5,3},{6,4},{7,5},{8,14},{9,15},{10,... | collective-permute-start | bytes 20 | tf_op jit(solution)/shard_map/ppermute | solution.py:95
  140.0 5.2 %collective-permute-start.6 = (f32[]{:T(128)}, f32[]{:T(128)}, u32[]{:S(2)}, u32[]{:S(2)}) collective-permute-start(f32[]{:T(128)} %add.259), channel_id=1, source_target_pairs={{0,7},{1,0},{2,1},{3,2},{4,3},{5,4},{6,5},{7,6},{8,15},{9,8},{10,9... | collective-permute-start | bytes 20 | tf_op jit(solution)/shard_map/ppermute | solution.py:95
  (5 other events, 5.9 us)

commit v2 on v0

--- a/solution.py
+++ b/solution.py
@@ -7,7 +7,7 @@
 
 radix_cols = 128
 block_limit = 64
-highest = lax.Precision.HIGHEST
+highest = lax.Precision.HIGH
 wide_type = jnp.float32
 narrow_type = jnp.bfloat16
 

time: 200 us -> 194 us (0.970)
  matrix products: 19.4 us -> 13.1 us
    dot_general x2, matrix products: 4.95 us -> 2.85 us  [inverse_dft(): jnp.einsum('kna,mkab->nmb', outer_table, twisted, precision=highest)]
    dot_general x2, matrix products: 4.4 us -> 2.35 us  [inverse_dft(): jnp.einsum('mkab,kjbq->mjaq', spectrum, inverse_inner, precision=highest)]
where the time goes in v2:
time: 194 us; the launch traced here: 193 us
  blocking collectives  53.6 us (28%)
  starting transfers between devices  43.3 us (22%)
  waiting for transfers between devices  37.9 us (20%)
  local copies, waits for them, and re-layouts  22.6 us (12%)
  other arithmetic  15.3 us (8%)
  matrix products  13.1 us (7%)
  between operations  6.9 us (4%)
    all_to_all x1, blocking collectives, body(): back = lax.all_to_all(returned, 'ctx', 0, 0, tiled=True)  53.6 us
    all_to_all x1, waiting for transfers between devices, body(): arrived = lax.all_to_all(outbound, 'ctx', 0, 0, tiled=True)  37.3 us
    all_to_all x1, starting transfers between devices, body(): arrived = lax.all_to_all(outbound, 'ctx', 0, 0, tiled=True)  21.7 us
    ppermute x3, starting transfers between devices, butterfly_sum(): value = value + lax.ppermute(value, axis, pairs)  21.5 us
    unnamed x57, local copies, waits for them, and re-layouts  11 us
  transfers between devices with their start and end apart: 4, of which 3 were waited for; matrix products, arithmetic and copies ran while one was open for 2% of the time, Pallas kernels for 0%

profile of v2, /device:TPU:1, one launch (start us, length us, event | category | flops | bytes accessed | tf_op | source)
XLA Modules:
  0.0 192.5 jit_solution(8885452066770770854)
XLA Ops:
  0.7 1.2 copy.74
  1.8 1.1 copy.75
  3.0 1.1 copy.76
  4.1 1.1 copy.77
  5.6 1.0 pad_maximum_fusion
  6.6 21.7 %all-to-all-start = ((bf16[64,49,128]{2,1,0:T(8,128)(2,1)}), bf16[64,49,128]{2,1,0:T(8,128)(2,1)S(1)}, u32[]{:S(2)}, u32[]{:S(2)}) async-start(bf16[64,49,128]{2,1,0:T(8,128)(2,1)} %pad_maximum_fusion), calls=%async_computation | async-start | bytes 1835008 | tf_op jit(solution)/shard_map/all_to_all | solution.py:232
  32.8 37.3 %all-to-all-done = bf16[64,49,128]{2,1,0:T(8,128)(2,1)S(1)} async-done(((bf16[64,49,128]{2,1,0:T(8,128)(2,1)}), bf16[64,49,128]{2,1,0:T(8,128)(2,1)S(1)}, u32[]{:S(2)}, u32[]{:S(2)}) %all-to-all-start) | async-done | bytes 802848 | tf_op jit(solution)/shard_map/all_to_all | solution.py:232
  70.9 1.0 fusion.33
  71.9 1.3 convolution_bitcast_fusion
  74.1 2.1 %fusion.12 = f32[32,2,128,128]{2,3,0,1:T(8,128)S(1)} fusion(f32[32,1,128,128]{2,3,1,0:T(8,128)S(1)} %get-tuple-element.55, f32[32,1,128,128]{2,3,1,0:T(8,128)S(1)} %get-tuple-element.54, f32[1,2,128,128]{2,3,0,1:T(8,128)S(1)} %get-tuple-element.81, f32[1,2,128,128]{2,3,0,1:T(8,128)S(1)} %get-tuple-element.88), kind=kOutput, calls=%fused_computation.12 | convolution fusion | flops 1611726848 | bytes 8650752 | tf_op jit(solution)/shard_map/mkab,kjbq->mjaq/dot_general | solution.py:59
  78.6 2.1 %fusion.9 = f32[32,2,128,128]{2,3,1,0:T(8,128)S(1)} fusion(f32[16,2,128,128]{2,3,0,1:T(8,128)S(1)} %maximum_bitcast_fusion.6, f32[16,2,128,128]{2,3,0,1:T(8,128)S(1)} %maximum_bitcast_fusion.5, f32[1,2,128,128]{2,3,1,0:T(8,128)S(1)} %get-tuple-element.89, f32[1,2,128,128]{2,3,1,0:T(8,128)S(1)} %get-tuple-element.80), kind=kOutput, calls=%fused_computation.11 | convolution fusion | flops 1611726848 | bytes 8650752 | tf_op jit(solution)/shard_map/mkab,kjbq->mjaq/dot_general | solution.py:64
  81.6 2.0 %fusion.19 = bf16[64,32,128]{2,0,1:T(8,128)(2,1)S(1)} fusion(f32[32,1,128,128]{2,3,1,0:T(8,128)S(1)} %get-tuple-element.53, f32[32,1,128,128]{2,3,1,0:T(8,128)S(1)} %get-tuple-element.52, f32[1,64,128]{2,1,0:T(8,128)S(1)} %copy-done.7, f32[1,64,128]{2,1,0:T(8,128)S(1)} %copy-done.10), kind=kOutput, calls=%fused_computation.25 | convolution fusion | flops 404242432 | bytes 4784128 | tf_op jit(solution)/shard_map/kna,mkab->nmb/dot_general | solution.py:74
  84.5 1.0 fusion.96
  87.7 1.7 copy.93
  89.4 1.0 copy.128
  91.4 1.9 reshape.555
  94.3 1.1 bitcast_convert_fusion
  101.2 6.3 %collective-permute-start = (f32[]{:T(128)}, f32[]{:T(128)}, u32[]{:S(2)}, u32[]{:S(2)}) collective-permute-start(f32[]{:T(128)} %add.224), channel_id=1, source_target_pairs={{0,1},{1,0},{2,3},{3,2},{4,5},{5,4},{6,7},{7,6},{8,9},{9,8},{10,11... | collective-permute-start | bytes 20 | tf_op jit(solution)/shard_map/ppermute | solution.py:93
  108.1 10.5 %collective-permute-start.1 = (f32[]{:T(128)}, f32[]{:T(128)}, u32[]{:S(2)}, u32[]{:S(2)}) collective-permute-start(f32[]{:T(128)} %add.225), channel_id=1, source_target_pairs={{0,2},{1,3},{2,0},{3,1},{4,6},{5,7},{6,4},{7,5},{8,10},{9,11},{10,... | collective-permute-start | bytes 20 | tf_op jit(solution)/shard_map/ppermute | solution.py:93
  119.4 4.7 %collective-permute-start.2 = (f32[]{:T(128)}, f32[]{:T(128)}, u32[]{:S(2)}, u32[]{:S(2)}) collective-permute-start(f32[]{:T(128)} %add.226), channel_id=1, source_target_pairs={{0,4},{1,5},{2,6},{3,7},{4,0},{5,1},{6,2},{7,3},{8,12},{9,13},{10,... | collective-permute-start | bytes 20 | tf_op jit(solution)/shard_map/ppermute | solution.py:93
  125.8 1.8 fusion.114
  127.7 1.3 scatter.9
  129.6 1.7 copy.94
  131.3 53.6 %all_to_all.10 = bf16[64,52,128]{2,1,0:T(8,128)(2,1)S(1)} all-to-all(bf16[64,52,128]{2,1,0:T(8,128)(2,1)S(1)} %copy.94), channel_id=1, replica_groups=mesh['ctx'=64,'ch'=8] {'ctx'}, dimensions={0} | all-to-all | bytes 1703936 | tf_op jit(solution)/shard_map/all_to_all | solution.py:245
  (110 shorter events, 25.9 us)
Async XLA Ops:
  0.6 27.7 %copy-start = (bf16[128,64]{0,1:T(8,128)(2,1)S(1)}, bf16[128,64]{0,1:T(8,128)(2,1)}, u32[]{:S(2)}) copy-start(bf16[128,64]{0,1:T(8,128)(2,1)} %param.16) | copy-start | bytes 49156
  0.6 4.6 %copy-start.16 = (bf16[128,1024]{1,0:T(8,128)(2,1)S(1)}, bf16[128,1024]{1,0:T(8,128)(2,1)}, u32[]{:S(2)}) copy-start(bf16[128,1024]{1,0:T(8,128)(2,1)} %param.12) | copy-start | bytes 786436
  0.7 4.7 %copy-start.17 = (bf16[128,64]{0,1:T(8,128)(2,1)S(1)}, bf16[128,64]{0,1:T(8,128)(2,1)}, u32[]{:S(2)}) copy-start(bf16[128,64]{0,1:T(8,128)(2,1)} %param.17) | copy-start | bytes 49156
  6.6 63.5 %all-to-all-start = ((bf16[64,49,128]{2,1,0:T(8,128)(2,1)}), bf16[64,49,128]{2,1,0:T(8,128)(2,1)S(1)}, u32[]{:S(2)}, u32[]{:S(2)}) async-start(bf16[64,49,128]{2,1,0:T(8,128)(2,1)} %pad_maximum_fusion), calls=%async_computation | async-start | bytes 1835008 | tf_op jit(solution)/shard_map/all_to_all | solution.py:232
  29.2 41.4 %copy-start.12 = (bf16[1,128,255]{2,1,0:T(8,128)(2,1)}, bf16[1,128,255]{2,1,0:T(8,128)(2,1)S(1)}, u32[]{:S(2)}) copy-start(bf16[1,128,255]{2,1,0:T(8,128)(2,1)S(1)} %reshape.541) | copy-start | bytes 195844
  31.9 44.5 %copy-start.6 = (f32[1,64,128]{2,1,0:T(8,128)}, f32[1,64,128]{2,1,0:T(8,128)S(1)}, u32[]{:S(2)}) copy-start(f32[1,64,128]{2,1,0:T(8,128)S(1)} %get-tuple-element.96) | copy-start | bytes 98308
  31.9 44.5 %copy-start.9 = (f32[1,64,128]{2,1,0:T(8,128)}, f32[1,64,128]{2,1,0:T(8,128)S(1)}, u32[]{:S(2)}) copy-start(f32[1,64,128]{2,1,0:T(8,128)S(1)} %get-tuple-element.97) | copy-start | bytes 98308
  32.8 45.8 %copy-start.3 = (f32[1,2,128,128]{2,3,1,0:T(8,128)}, f32[1,2,128,128]{2,3,1,0:T(8,128)S(1)}, u32[]{:S(2)}) copy-start(f32[1,2,128,128]{2,3,1,0:T(8,128)S(1)} %get-tuple-element.89) | copy-start | bytes 393220
  70.1 0.8 copy-start.14
  80.7 0.9 copy-start.7
  80.7 0.9 copy-start.10
  81.6 2.9 %copy-start.13 = (bf16[1,128,255]{2,1,0:T(8,128)(2,1)S(1)}, bf16[1,128,255]{2,1,0:T(8,128)(2,1)}, u32[]{:S(2)}) copy-start(bf16[1,128,255]{2,1,0:T(8,128)(2,1)} %copy-done.12) | copy-start | bytes 195844
  93.3 2.8 %copy-start.4 = (f32[1,2,128,128]{2,3,1,0:T(8,128)S(1)}, f32[1,2,128,128]{2,3,1,0:T(8,128)}, u32[]{:S(2)}) copy-start(f32[1,2,128,128]{2,3,1,0:T(8,128)} %copy-done.3) | copy-start | bytes 393220
  93.3 3.4 %copy-start.1 = (f32[64,16,128]{2,0,1:T(8,128)S(1)}, f32[64,16,128]{2,0,1:T(8,128)}, u32[]{:S(2)}) copy-start(f32[64,16,128]{2,0,1:T(8,128)} %get-tuple-element.93) | copy-start | bytes 1572868
  93.3 4.2 %copy-start.2 = (f32[128,64,16]{0,1,2:T(8,128)S(1)}, f32[128,64,16]{0,1,2:T(8,128)}, u32[]{:S(2)}) copy-start(f32[128,64,16]{0,1,2:T(8,128)} %fusion.96) | copy-start | bytes 1572868
  93.3 4.2 %copy-start.5 = (bf16[63,1,16,128]{3,0,2,1:T(8,128)(2,1)S(1)}, bf16[63,1,16,128]{3,0,2,1:T(8,128)(2,1)}, u32[]{:S(2)}) copy-start(bf16[63,1,16,128]{3,0,2,1:T(8,128)(2,1)} %slice_bitcast_fusion.2) | copy-start | bytes 774148
  93.3 4.2 %copy-start.15 = (bf16[1,128,127]{2,1,0:T(8,128)(2,1)S(1)}, bf16[1,128,127]{2,1,0:T(8,128)(2,1)}, u32[]{:S(2)}) copy-start(bf16[1,128,127]{2,1,0:T(8,128)(2,1)} %slice.199) | copy-start | bytes 97540
  96.0 2.4 %copy-start.8 = (f32[1,64,128]{2,1,0:T(8,128)S(1)}, f32[1,64,128]{2,1,0:T(8,128)}, u32[]{:S(2)}) copy-start(f32[1,64,128]{2,1,0:T(8,128)} %copy-done.6) | copy-start | bytes 98308
  96.0 2.4 %copy-start.11 = (f32[1,64,128]{2,1,0:T(8,128)S(1)}, f32[1,64,128]{2,1,0:T(8,128)}, u32[]{:S(2)}) copy-start(f32[1,64,128]{2,1,0:T(8,128)} %copy-done.9) | copy-start | bytes 98308
  96.1 32.9 %copy-start.18 = (bf16[1,128]{1,0:T(2,128)(2,1)S(1)}, bf16[1,128]{1,0:T(2,128)(2,1)}, u32[]{:S(2)}) copy-start(bf16[1,128]{1,0:T(2,128)(2,1)} %get-tuple-element.90) | copy-start | bytes 772
  96.1 32.9 %copy-start.19 = (bf16[1,128]{1,0:T(2,128)(2,1)S(1)}, bf16[1,128]{1,0:T(2,128)(2,1)}, u32[]{:S(2)}) copy-start(bf16[1,128]{1,0:T(2,128)(2,1)} %fusion.100) | copy-start | bytes 772
  101.2 6.3 %collective-permute-start = (f32[]{:T(128)}, f32[]{:T(128)}, u32[]{:S(2)}, u32[]{:S(2)}) collective-permute-start(f32[]{:T(128)} %add.224), channel_id=1, source_target_pairs={{0,1},{1,0},{2,3},{3,2},{4,5},{5,4},{6,7},{7,6},{8,9},{9,8},{10,11... | collective-permute-start | bytes 20 | tf_op jit(solution)/shard_map/ppermute | solution.py:93
  108.1 10.6 %collective-permute-start.1 = (f32[]{:T(128)}, f32[]{:T(128)}, u32[]{:S(2)}, u32[]{:S(2)}) collective-permute-start(f32[]{:T(128)} %add.225), channel_id=1, source_target_pairs={{0,2},{1,3},{2,0},{3,1},{4,6},{5,7},{6,4},{7,5},{8,10},{9,11},{10,... | collective-permute-start | bytes 20 | tf_op jit(solution)/shard_map/ppermute | solution.py:93
  119.4 5.1 %collective-permute-start.2 = (f32[]{:T(128)}, f32[]{:T(128)}, u32[]{:S(2)}, u32[]{:S(2)}) collective-permute-start(f32[]{:T(128)} %add.226), channel_id=1, source_target_pairs={{0,4},{1,5},{2,6},{3,7},{4,0},{5,1},{6,2},{7,3},{8,12},{9,13},{10,... | collective-permute-start | bytes 20 | tf_op jit(solution)/shard_map/ppermute | solution.py:93

commit v3 on v1

--- a/solution.py
+++ b/solution.py
@@ -7,7 +7,7 @@
 
 radix_cols = 128
 block_limit = 64
-highest = lax.Precision.HIGHEST
+highest = lax.Precision.HIGH
 wide_type = jnp.float32
 narrow_type = jnp.bfloat16
 
@@ -83,18 +83,6 @@
 
 def joined_wide(high, low):
     return high.astype(wide_type) + low.astype(wide_type)
-
-
-def gathered_sum(value, axis):
-    peers = lax.axis_size(axis)
-    source = lax.axis_index(axis)
-    slot_ids = lax.iota(jnp.int32, peers)
-    slots = jnp.where(slot_ids == source, value, 0.0)
-    for shift in range(1, peers):
-        pairs = [(i, (i + shift) % peers) for i in range(peers)]
-        got = lax.ppermute(value, axis, pairs)
-        slots = slots + jnp.where(slot_ids == (source - shift) % peers, got, 0.0)
-    return jnp.sum(slots)
 
 
 def medium_bands(filt):
@@ -194,7 +182,7 @@
     ).reshape(item_count, tap_count, 2 * tap_count + 1)
     grad_medium = jnp.sum(lag_table[:, :, :tap_count], axis=1) * scale
     squares = jnp.sum(jnp.square(lagged.astype(wide_type))) + jnp.sum(grad_medium * grad_medium)
-    squares = gathered_sum(squares, "ch")
+    squares = lax.psum(squares, "ch")
     medium_high, medium_low = split_wide(grad_medium)
     squares_high, squares_low = split_wide(squares)
     squares_row = jnp.concatenate(

time: 216 us -> 191 us (0.88)
  starting transfers between devices: 59.5 us -> 21.7 us
  blocking collectives: 53.8 us -> 78.7 us
  matrix products: 19.3 us -> 13 us
  other arithmetic: 16.6 us -> 11.7 us
    ppermute x7 -> x0, starting transfers between devices: 37.7 us -> none  [gathered_sum(): got = lax.ppermute(value, axis, pairs)]
    psum x0 -> x1, blocking collectives: none -> 21 us  [channel_work(): squares = lax.psum(squares, 'ch')]
    reduce_sum x1 -> x0, other arithmetic: 4.98 us -> none  [gathered_sum(): return jnp.sum(slots)]
    all_to_all x1, blocking collectives: 53.8 us -> 57.7 us  [body(): back = lax.all_to_all(returned, 'ctx', 0, 0, tiled=True)]
  transfers between devices with their start and end apart: 8 -> 1, of which waited for: 2 -> 1; matrix products, arithmetic and copies ran while one was open for 1% -> 1% of each run, Pallas kernels for 0% -> 0%
where the time goes in v3:
time: 191 us
  blocking collectives  78.7 us (41%)
  waiting for transfers between devices  39.2 us (21%)
  starting transfers between devices  21.7 us (11%)
  local copies, waits for them, and re-layouts  20.7 us (11%)
  matrix products  13 us (7%)
  other arithmetic  11.7 us (6%)
  between operations  5.62 us (3%)
    all_to_all x1, blocking collectives, body(): back = lax.all_to_all(returned, 'ctx', 0, 0, tiled=True)  57.7 us
    all_to_all x1, waiting for transfers between devices, body(): arrived = lax.all_to_all(outbound, 'ctx', 0, 0, tiled=True)  39.2 us
    all_to_all x1, starting transfers between devices, body(): arrived = lax.all_to_all(outbound, 'ctx', 0, 0, tiled=True)  21.7 us
    psum x1, blocking collectives, channel_work(): squares = lax.psum(squares, 'ch')  21 us
    unnamed x59, local copies, waits for them, and re-layouts  11 us
  transfers between devices with their start and end apart: 1, of which 1 were waited for; matrix products, arithmetic and copies ran while one was open for 1% of the time, Pallas kernels for 0%

profile of v3, /device:TPU:1, one launch (start us, length us, event | category | flops | bytes accessed | tf_op | source)
XLA Modules:
  0.0 190.7 jit_solution(17172195198591536070)
XLA Ops:
  0.7 1.2 copy.74
  1.8 1.1 copy.75
  3.0 1.1 copy.76
  4.1 1.1 copy.77
  5.6 1.0 pad_maximum_fusion
  6.6 21.7 %all-to-all-start = ((bf16[64,49,128]{2,1,0:T(8,128)(2,1)}), bf16[64,49,128]{2,1,0:T(8,128)(2,1)S(1)}, u32[]{:S(2)}, u32[]{:S(2)}) async-start(bf16[64,49,128]{2,1,0:T(8,128)(2,1)} %pad_maximum_fusion), calls=%async_computation | async-start | bytes 1835008 | tf_op jit(solution)/shard_map/all_to_all | solution.py:228
  30.9 39.2 %all-to-all-done = bf16[64,49,128]{2,1,0:T(8,128)(2,1)S(1)} async-done(((bf16[64,49,128]{2,1,0:T(8,128)(2,1)}), bf16[64,49,128]{2,1,0:T(8,128)(2,1)S(1)}, u32[]{:S(2)}, u32[]{:S(2)}) %all-to-all-start) | async-done | bytes 802848 | tf_op jit(solution)/shard_map/all_to_all | solution.py:228
  70.9 1.0 fusion.33
  71.9 1.3 convolution_bitcast_fusion
  74.1 2.1 %fusion.12 = f32[32,2,128,128]{2,3,0,1:T(8,128)S(1)} fusion(f32[32,1,128,128]{2,3,1,0:T(8,128)S(1)} %get-tuple-element.31, f32[32,1,128,128]{2,3,1,0:T(8,128)S(1)} %get-tuple-element.30, f32[1,2,128,128]{2,3,0,1:T(8,128)S(1)} %get-tuple-element.57, f32[1,2,128,128]{2,3,0,1:T(8,128)S(1)} %get-tuple-element.64), kind=kOutput, calls=%fused_computation.12 | convolution fusion | flops 1611726848 | bytes 8650752 | tf_op jit(solution)/shard_map/mkab,kjbq->mjaq/dot_general | solution.py:59
  77.3 1.0 multiply_add_fusion.2
  78.6 2.1 %fusion.9 = f32[32,2,128,128]{2,3,1,0:T(8,128)S(1)} fusion(f32[16,2,128,128]{2,3,0,1:T(8,128)S(1)} %maximum_bitcast_fusion.6, f32[16,2,128,128]{2,3,0,1:T(8,128)S(1)} %maximum_bitcast_fusion.5, f32[1,2,128,128]{2,3,1,0:T(8,128)S(1)} %get-tuple-element.65, f32[1,2,128,128]{2,3,1,0:T(8,128)S(1)} %get-tuple-element.56), kind=kOutput, calls=%fused_computation.11 | convolution fusion | flops 1611726848 | bytes 8650752 | tf_op jit(solution)/shard_map/mkab,kjbq->mjaq/dot_general | solution.py:64
  81.6 2.2 %fusion.19 = bf16[64,32,128]{2,0,1:T(8,128)(2,1)S(1)} fusion(f32[32,1,128,128]{2,3,1,0:T(8,128)S(1)} %get-tuple-element.29, f32[32,1,128,128]{2,3,1,0:T(8,128)S(1)} %get-tuple-element.28, f32[1,64,128]{2,1,0:T(8,128)S(1)} %copy-done.7, f32[1,64,128]{2,1,0:T(8,128)S(1)} %copy-done.10), kind=kOutput, calls=%fused_computation.25 | convolution fusion | flops 404242432 | bytes 4784128 | tf_op jit(solution)/shard_map/kna,mkab->nmb/dot_general | solution.py:74
  84.5 1.0 fusion.96
  87.7 1.7 copy.93
  89.3 1.0 copy.128
  90.4 1.0 pad_reduce_fusion
  91.3 1.9 %reshape.497 = f32[1,128,257]{2,1,0:T(8,128)} reshape(f32[32896]{0:T(1024)} %pad_reduce_fusion) | data formatting | bytes 263168 | tf_op jit(solution)/shard_map/reshape | solution.py:182
  93.3 1.0 slice_reduce_fusion.1
  94.3 1.1 bitcast_convert_fusion
  96.9 0.9 fusion.25
  100.6 21.0 %psum.7 = f32[]{:T(128)} all-reduce(f32[]{:T(128)S(6)} %add.211), channel_id=1, replica_groups=mesh['ctx'=64,'ch'=8] {'ch'}, use_global_device_ids=true, to_apply=%region_4.5 | all-reduce | flops 1 | bytes 8 | tf_op jit(solution)/shard_map/psum | solution.py:185
  123.6 1.7 copy.94
  125.3 57.7 %all_to_all.10 = bf16[64,52,128]{2,1,0:T(8,128)(2,1)S(1)} all-to-all(bf16[64,52,128]{2,1,0:T(8,128)(2,1)S(1)} %copy.94), channel_id=1, replica_groups=mesh['ctx'=64,'ch'=8] {'ctx'}, dimensions={0} | all-to-all | bytes 1703936 | tf_op jit(solution)/shard_map/all_to_all | solution.py:241
  (101 shorter events, 18.8 us)
Async XLA Ops:
  0.6 27.7 %copy-start = (bf16[128,64]{0,1:T(8,128)(2,1)S(1)}, bf16[128,64]{0,1:T(8,128)(2,1)}, u32[]{:S(2)}) copy-start(bf16[128,64]{0,1:T(8,128)(2,1)} %param.12) | copy-start | bytes 49156
  0.6 4.6 %copy-start.16 = (bf16[128,1024]{1,0:T(8,128)(2,1)S(1)}, bf16[128,1024]{1,0:T(8,128)(2,1)}, u32[]{:S(2)}) copy-start(bf16[128,1024]{1,0:T(8,128)(2,1)} %param.8) | copy-start | bytes 786436
  0.7 4.7 %copy-start.17 = (bf16[128,64]{0,1:T(8,128)(2,1)S(1)}, bf16[128,64]{0,1:T(8,128)(2,1)}, u32[]{:S(2)}) copy-start(bf16[128,64]{0,1:T(8,128)(2,1)} %param.13) | copy-start | bytes 49156
  6.6 63.5 %all-to-all-start = ((bf16[64,49,128]{2,1,0:T(8,128)(2,1)}), bf16[64,49,128]{2,1,0:T(8,128)(2,1)S(1)}, u32[]{:S(2)}, u32[]{:S(2)}) async-start(bf16[64,49,128]{2,1,0:T(8,128)(2,1)} %pad_maximum_fusion), calls=%async_computation | async-start | bytes 1835008 | tf_op jit(solution)/shard_map/all_to_all | solution.py:228
  29.2 41.4 %copy-start.12 = (bf16[1,128,255]{2,1,0:T(8,128)(2,1)}, bf16[1,128,255]{2,1,0:T(8,128)(2,1)S(1)}, u32[]{:S(2)}) copy-start(bf16[1,128,255]{2,1,0:T(8,128)(2,1)S(1)} %reshape.483) | copy-start | bytes 195844
  30.0 46.5 %copy-start.6 = (f32[1,64,128]{2,1,0:T(8,128)}, f32[1,64,128]{2,1,0:T(8,128)S(1)}, u32[]{:S(2)}) copy-start(f32[1,64,128]{2,1,0:T(8,128)S(1)} %get-tuple-element.72) | copy-start | bytes 98308
  30.0 46.5 %copy-start.9 = (f32[1,64,128]{2,1,0:T(8,128)}, f32[1,64,128]{2,1,0:T(8,128)S(1)}, u32[]{:S(2)}) copy-start(f32[1,64,128]{2,1,0:T(8,128)S(1)} %get-tuple-element.73) | copy-start | bytes 98308
  30.9 47.7 %copy-start.3 = (f32[1,2,128,128]{2,3,1,0:T(8,128)}, f32[1,2,128,128]{2,3,1,0:T(8,128)S(1)}, u32[]{:S(2)}) copy-start(f32[1,2,128,128]{2,3,1,0:T(8,128)S(1)} %get-tuple-element.65) | copy-start | bytes 393220
  70.1 0.8 copy-start.14
  80.7 0.9 copy-start.7
  80.7 0.9 copy-start.10
  81.6 2.9 %copy-start.13 = (bf16[1,128,255]{2,1,0:T(8,128)(2,1)S(1)}, bf16[1,128,255]{2,1,0:T(8,128)(2,1)}, u32[]{:S(2)}) copy-start(bf16[1,128,255]{2,1,0:T(8,128)(2,1)} %copy-done.12) | copy-start | bytes 195844
  93.3 2.2 %copy-start.4 = (f32[1,2,128,128]{2,3,1,0:T(8,128)S(1)}, f32[1,2,128,128]{2,3,1,0:T(8,128)}, u32[]{:S(2)}) copy-start(f32[1,2,128,128]{2,3,1,0:T(8,128)} %copy-done.3) | copy-start | bytes 393220
  93.3 2.8 %copy-start.1 = (f32[64,16,128]{2,0,1:T(8,128)S(1)}, f32[64,16,128]{2,0,1:T(8,128)}, u32[]{:S(2)}) copy-start(f32[64,16,128]{2,0,1:T(8,128)} %get-tuple-element.69) | copy-start | bytes 1572868
  93.3 3.6 %copy-start.2 = (f32[128,64,16]{0,1,2:T(8,128)S(1)}, f32[128,64,16]{0,1,2:T(8,128)}, u32[]{:S(2)}) copy-start(f32[128,64,16]{0,1,2:T(8,128)} %fusion.96) | copy-start | bytes 1572868
  93.3 3.6 %copy-start.5 = (bf16[63,1,16,128]{3,0,2,1:T(8,128)(2,1)S(1)}, bf16[63,1,16,128]{3,0,2,1:T(8,128)(2,1)}, u32[]{:S(2)}) copy-start(bf16[63,1,16,128]{3,0,2,1:T(8,128)(2,1)} %slice_bitcast_fusion.2) | copy-start | bytes 774148
  93.3 3.6 %copy-start.15 = (bf16[1,128,127]{2,1,0:T(8,128)(2,1)S(1)}, bf16[1,128,127]{2,1,0:T(8,128)(2,1)}, u32[]{:S(2)}) copy-start(bf16[1,128,127]{2,1,0:T(8,128)(2,1)} %slice.163) | copy-start | bytes 97540
  94.3 1.1 copy-start.18
  95.4 2.5 %copy-start.8 = (f32[1,64,128]{2,1,0:T(8,128)S(1)}, f32[1,64,128]{2,1,0:T(8,128)}, u32[]{:S(2)}) copy-start(f32[1,64,128]{2,1,0:T(8,128)} %copy-done.6) | copy-start | bytes 98308
  95.4 2.5 %copy-start.11 = (f32[1,64,128]{2,1,0:T(8,128)S(1)}, f32[1,64,128]{2,1,0:T(8,128)}, u32[]{:S(2)}) copy-start(f32[1,64,128]{2,1,0:T(8,128)} %copy-done.9) | copy-start | bytes 98308
  95.5 5.1 %copy-start.19 = (f32[128]{0:T(128)S(1)}, f32[128]{0:T(128)}, u32[]{:S(2)}) copy-start(f32[128]{0:T(128)} %copy-done.18) | copy-start | bytes 1540
  95.5 27.4 %copy-start.20 = (bf16[1,128]{1,0:T(2,128)(2,1)S(1)}, bf16[1,128]{1,0:T(2,128)(2,1)}, u32[]{:S(2)}) copy-start(bf16[1,128]{1,0:T(2,128)(2,1)} %get-tuple-element.66) | copy-start | bytes 772

commit v4 on v3

--- a/solution.py
+++ b/solution.py
@@ -182,22 +182,13 @@
     ).reshape(item_count, tap_count, 2 * tap_count + 1)
     grad_medium = jnp.sum(lag_table[:, :, :tap_count], axis=1) * scale
     squares = jnp.sum(jnp.square(lagged.astype(wide_type))) + jnp.sum(grad_medium * grad_medium)
-    squares = lax.psum(squares, "ch")
     medium_high, medium_low = split_wide(grad_medium)
-    squares_high, squares_low = split_wide(squares)
-    squares_row = jnp.concatenate(
-        [
-            squares_high.reshape(1, 1),
-            squares_low.reshape(1, 1),
-            jnp.zeros((1, radix_cols - 2), narrow_type),
-        ],
-        axis=1,
-    )
-    shared = jnp.concatenate([medium_high, medium_low, squares_row], axis=0)
+    shared = jnp.concatenate([medium_high, medium_low], axis=0)
     shared = jnp.broadcast_to(shared[None], (half_rows,) + shared.shape)
-    return jnp.concatenate(
+    stacked = jnp.concatenate(
         [second_mix, grad_second, grad_gated.astype(narrow_type), lagged, shared], axis=1
     )
+    return stacked, squares
 
 
 def body(first_gate, second_gate, output_gate, values, cotangent, medium_filter, long_filter):
@@ -229,7 +220,7 @@
     own_filter = lax.dynamic_slice_in_dim(
         medium_filter, lax.axis_index("ctx") * ctx_groups, ctx_groups, axis=1
     )
-    returned = channel_work(
+    returned, squares = channel_work(
         (
             arrived[:, :chan_share],
             arrived[:, chan_share : 2 * chan_share],
@@ -251,8 +242,8 @@
         token_rows(3 * chan_share + ctx_groups, ctx_groups),
         token_rows(3 * chan_share + 2 * ctx_groups, ctx_groups),
     )
-    squares_row = back[:, 3 * chan_share + 3 * ctx_groups]
-    total_squares = jnp.sum(joined_wide(squares_row[:, 0], squares_row[:, 1]))
+    every_squares = lax.all_gather(squares.reshape(1), ("ctx", "ch"), tiled=True)
+    total_squares = jnp.sum(every_squares)
     grad_output_gate = (cotangent_wide * second_mix.astype(wide_type)).astype(narrow_type)
     grad_first = (grad_gated * values_wide).astype(narrow_type)
     grad_values = (grad_gated * first_wide).astype(narrow_type)

time: 191 us -> 237 us (1.24)
  blocking collectives: 78.7 us -> 114 us
  starting transfers between devices: 21.7 us -> 36.6 us
    unnamed x0 -> x1, blocking collectives: none -> 114 us
    all_to_all x1 -> x0, blocking collectives: 57.7 us -> none  [body(): back = lax.all_to_all(returned, 'ctx', 0, 0, tiled=True)]
    psum x1 -> x0, blocking collectives: 21 us -> none  [channel_work(): squares = lax.psum(squares, 'ch')]
    all_to_all x0 -> x1, starting transfers between devices: none -> 14.9 us  [body(): back = lax.all_to_all(returned, 'ctx', 0, 0, tiled=True)]
    unnamed x59 -> x56, local copies, waits for them, and re-layouts: 11 us -> 11.1 us
  transfers between devices with their start and end apart: 1 -> 2, of which waited for: 1 -> 1; matrix products, arithmetic and copies ran while one was open for 1% -> 2% of each run, Pallas kernels for 0% -> 0%
where the time goes in v4:
time: 237 us; the launch traced here: 236 us
  blocking collectives  114 us (48%)
  waiting for transfers between devices  39.2 us (17%)
  starting transfers between devices  36.6 us (15%)
  local copies, waits for them, and re-layouts  19.9 us (8%)
  matrix products  11.8 us (5%)
  other arithmetic  10.3 us (4%)
  between operations  4.37 us (2%)
    unnamed x1, blocking collectives  114 us
    all_to_all x1, waiting for transfers between devices, body(): arrived = lax.all_to_all(outbound, 'ctx', 0, 0, tiled=True)  39.2 us
    all_to_all x1, starting transfers between devices, body(): arrived = lax.all_to_all(outbound, 'ctx', 0, 0, tiled=True)  21.7 us
    all_to_all x1, starting transfers between devices, body(): back = lax.all_to_all(returned, 'ctx', 0, 0, tiled=True)  14.9 us
    unnamed x56, local copies, waits for them, and re-layouts  11.1 us
  transfers between devices with their start and end apart: 2, of which 1 were waited for; matrix products, arithmetic and copies ran while one was open for 2% of the time, Pallas kernels for 0%

profile of v4, /device:TPU:1, one launch (start us, length us, event | category | flops | bytes accessed | tf_op | source)
XLA Modules:
  0.0 236.2 jit_solution(3039325417827905982)
XLA Ops:
  0.7 1.2 copy.74
  1.8 1.1 copy.75
  3.0 1.1 copy.76
  4.1 1.1 copy.77
  5.6 1.0 pad_maximum_fusion
  6.6 21.7 %all-to-all-start = ((bf16[64,49,128]{2,1,0:T(8,128)(2,1)}), bf16[64,49,128]{2,1,0:T(8,128)(2,1)S(1)}, u32[]{:S(2)}, u32[]{:S(2)}) async-start(bf16[64,49,128]{2,1,0:T(8,128)(2,1)} %pad_maximum_fusion), calls=%async_computation | async-start | bytes 1835008 | tf_op jit(solution)/shard_map/all_to_all | solution.py:219
  30.9 39.2 %all-to-all-done = bf16[64,49,128]{2,1,0:T(8,128)(2,1)S(1)} async-done(((bf16[64,49,128]{2,1,0:T(8,128)(2,1)}), bf16[64,49,128]{2,1,0:T(8,128)(2,1)S(1)}, u32[]{:S(2)}, u32[]{:S(2)}) %all-to-all-start) | async-done | bytes 802848 | tf_op jit(solution)/shard_map/all_to_all | solution.py:219
  70.9 1.0 fusion.33
  71.9 1.3 convolution_bitcast_fusion
  74.1 2.1 fusion.12
  77.3 1.0 multiply_add_fusion.2
  78.6 2.1 fusion.9
  81.6 2.2 fusion.19
  84.5 1.0 fusion.96
  87.7 1.7 copy.93
  89.3 1.0 copy.126
  90.4 1.0 pad_reduce_fusion
  91.4 1.9 reshape.491
  93.3 1.0 slice_reduce_fusion.1
  96.3 1.5 copy.94
  97.8 14.9 %all-to-all-start.1 = ((bf16[64,51,128]{2,1,0:T(8,128)(2,1)}), bf16[64,51,128]{2,1,0:T(8,128)(2,1)S(1)}, u32[]{:S(2)}, u32[]{:S(2)}) async-start(bf16[64,51,128]{2,1,0:T(8,128)(2,1)} %copy.94), calls=%async_computation.1 | async-start | bytes 1835008 | tf_op jit(solution)/shard_map/all_to_all | solution.py:232
  114.8 113.9 %all-reduce.5 = f32[512]{0:T(512)S(1)} all-reduce(f32[512]{0:T(512)S(1)} %dynamic-update-slice), channel_id=1, replica_groups=mesh['ctx'=64,'ch'=8] {'ctx','ch'}, use_global_device_ids=true, to_apply=%add.5 | all-reduce | flops 512 | bytes 4096
  230.3 0.8 copy.96
  232.1 0.8 copy.98
  (98 shorter events, 16.0 us)
Async XLA Ops:
  0.6 27.7 %copy-start = (bf16[128,64]{0,1:T(8,128)(2,1)S(1)}, bf16[128,64]{0,1:T(8,128)(2,1)}, u32[]{:S(2)}) copy-start(bf16[128,64]{0,1:T(8,128)(2,1)} %param.12) | copy-start | bytes 49156
  0.6 4.6 %copy-start.17 = (bf16[128,1024]{1,0:T(8,128)(2,1)S(1)}, bf16[128,1024]{1,0:T(8,128)(2,1)}, u32[]{:S(2)}) copy-start(bf16[128,1024]{1,0:T(8,128)(2,1)} %param.8) | copy-start | bytes 786436
  0.7 4.7 %copy-start.18 = (bf16[128,64]{0,1:T(8,128)(2,1)S(1)}, bf16[128,64]{0,1:T(8,128)(2,1)}, u32[]{:S(2)}) copy-start(bf16[128,64]{0,1:T(8,128)(2,1)} %param.13) | copy-start | bytes 49156
  6.6 63.5 %all-to-all-start = ((bf16[64,49,128]{2,1,0:T(8,128)(2,1)}), bf16[64,49,128]{2,1,0:T(8,128)(2,1)S(1)}, u32[]{:S(2)}, u32[]{:S(2)}) async-start(bf16[64,49,128]{2,1,0:T(8,128)(2,1)} %pad_maximum_fusion), calls=%async_computation | async-start | bytes 1835008 | tf_op jit(solution)/shard_map/all_to_all | solution.py:219
  29.2 41.4 %copy-start.13 = (bf16[1,128,255]{2,1,0:T(8,128)(2,1)}, bf16[1,128,255]{2,1,0:T(8,128)(2,1)S(1)}, u32[]{:S(2)}) copy-start(bf16[1,128,255]{2,1,0:T(8,128)(2,1)S(1)} %reshape.477) | copy-start | bytes 195844
  30.0 46.5 %copy-start.7 = (f32[1,64,128]{2,1,0:T(8,128)}, f32[1,64,128]{2,1,0:T(8,128)S(1)}, u32[]{:S(2)}) copy-start(f32[1,64,128]{2,1,0:T(8,128)S(1)} %get-tuple-element.70) | copy-start | bytes 98308
  30.0 46.5 %copy-start.10 = (f32[1,64,128]{2,1,0:T(8,128)}, f32[1,64,128]{2,1,0:T(8,128)S(1)}, u32[]{:S(2)}) copy-start(f32[1,64,128]{2,1,0:T(8,128)S(1)} %get-tuple-element.71) | copy-start | bytes 98308
  30.9 47.7 %copy-start.4 = (f32[1,2,128,128]{2,3,1,0:T(8,128)}, f32[1,2,128,128]{2,3,1,0:T(8,128)S(1)}, u32[]{:S(2)}) copy-start(f32[1,2,128,128]{2,3,1,0:T(8,128)S(1)} %get-tuple-element.63) | copy-start | bytes 393220
  70.1 0.8 copy-start.15
  80.7 0.9 copy-start.8
  80.7 0.9 copy-start.11
  81.6 2.9 %copy-start.14 = (bf16[1,128,255]{2,1,0:T(8,128)(2,1)S(1)}, bf16[1,128,255]{2,1,0:T(8,128)(2,1)}, u32[]{:S(2)}) copy-start(bf16[1,128,255]{2,1,0:T(8,128)(2,1)} %copy-done.13) | copy-start | bytes 195844
  93.3 1.8 copy-start.5
  93.3 2.4 copy-start.1
  93.3 2.4 %copy-start.3 = (bf16[64,51,128]{2,0,1:T(8,128)(2,1)S(1)}, bf16[64,51,128]{2,0,1:T(8,128)(2,1)}, u32[]{:S(2)}) copy-start(bf16[64,51,128]{2,0,1:T(8,128)(2,1)} %slice_dynamic-update-slice_fusion) | copy-start | bytes 2506756
  93.3 2.5 %copy-start.2 = (f32[128,64,16]{0,1,2:T(8,128)S(1)}, f32[128,64,16]{0,1,2:T(8,128)}, u32[]{:S(2)}) copy-start(f32[128,64,16]{0,1,2:T(8,128)} %fusion.96) | copy-start | bytes 1572868
  93.3 2.5 %copy-start.6 = (bf16[63,1,16,128]{3,0,2,1:T(8,128)(2,1)S(1)}, bf16[63,1,16,128]{3,0,2,1:T(8,128)(2,1)}, u32[]{:S(2)}) copy-start(bf16[63,1,16,128]{3,0,2,1:T(8,128)(2,1)} %slice_bitcast_fusion.2) | copy-start | bytes 774148
  93.3 2.5 %copy-start.16 = (bf16[1,128,127]{2,1,0:T(8,128)(2,1)S(1)}, bf16[1,128,127]{2,1,0:T(8,128)(2,1)}, u32[]{:S(2)}) copy-start(bf16[1,128,127]{2,1,0:T(8,128)(2,1)} %slice.151) | copy-start | bytes 97540
  94.9 1.1 copy-start.9
  94.9 1.1 copy-start.12
  97.8 132.2 %all-to-all-start.1 = ((bf16[64,51,128]{2,1,0:T(8,128)(2,1)}), bf16[64,51,128]{2,1,0:T(8,128)(2,1)S(1)}, u32[]{:S(2)}, u32[]{:S(2)}) async-start(bf16[64,51,128]{2,1,0:T(8,128)(2,1)} %copy.94), calls=%async_computation.1 | async-start | bytes 1835008 | tf_op jit(solution)/shard_map/all_to_all | solution.py:232

commit v5 on v3

--- a/solution.py
+++ b/solution.py
@@ -176,11 +176,15 @@
     prev_lags = jnp.einsum(
         "ngcs,ngcr->gsr", gated_prev, mixed_items, preferred_element_type=wide_type
     )
-    lag_table = jnp.concatenate([own_lags, prev_lags], axis=2).reshape(item_count, -1)
-    lag_table = jnp.concatenate(
-        [lag_table, jnp.zeros((item_count, tap_count), wide_type)], axis=1
-    ).reshape(item_count, tap_count, 2 * tap_count + 1)
-    grad_medium = jnp.sum(lag_table[:, :, :tap_count], axis=1) * scale
+    lag_table = jnp.concatenate([own_lags, prev_lags], axis=2)
+    lag_of = lax.broadcasted_iota(jnp.int32, (tap_count, tap_count, 2 * tap_count), 2) - (
+        lax.broadcasted_iota(jnp.int32, (tap_count, tap_count, 2 * tap_count), 1)
+    )
+    lag_ids = lax.broadcasted_iota(jnp.int32, (tap_count, tap_count, 2 * tap_count), 0)
+    on_lag = lag_of == lag_ids
+    grad_medium = (
+        jnp.sum(jnp.where(on_lag[None], lag_table[:, None], 0.0), axis=(2, 3)) * scale
+    )
     squares = jnp.sum(jnp.square(lagged.astype(wide_type))) + jnp.sum(grad_medium * grad_medium)
     squares = lax.psum(squares, "ch")
     medium_high, medium_low = split_wide(grad_medium)

time: 191 us -> 189 us (0.990)
  local copies, waits for them, and re-layouts: 20.7 us -> 16.8 us
    concatenate x2 -> x0, local copies, waits for them, and re-layouts: 2.65 us -> none  [the longest x1 1.66 us: channel_work(): jnp.concatenate([own_lags, prev_lags], axis=2).reshape(item_count, -1)]
    reshape x1 -> x0, local copies, waits for them, and re-layouts: 1.92 us -> none  [channel_work(): lag_table = jnp.concatenate([lag_table, jnp.zeros((item_count, tap_count)...]
    unnamed x59 -> x56, local copies, waits for them, and re-layouts: 11 us -> 9.97 us
where the time goes in v5:
time: 189 us
  blocking collectives  78.7 us (42%)
  waiting for transfers between devices  39.2 us (21%)
  starting transfers between devices  21.7 us (11%)
  local copies, waits for them, and re-layouts  16.8 us (9%)
  other arithmetic  13.6 us (7%)
  matrix products  13 us (7%)
  between operations  5.6 us (3%)
    all_to_all x1, blocking collectives, body(): back = lax.all_to_all(returned, 'ctx', 0, 0, tiled=True)  57.7 us
    all_to_all x1, waiting for transfers between devices, body(): arrived = lax.all_to_all(outbound, 'ctx', 0, 0, tiled=True)  39.2 us
    all_to_all x1, starting transfers between devices, body(): arrived = lax.all_to_all(outbound, 'ctx', 0, 0, tiled=True)  21.7 us
    psum x1, blocking collectives, channel_work(): squares = lax.psum(squares, 'ch')  20.9 us
    unnamed x56, local copies, waits for them, and re-layouts  9.97 us
  transfers between devices with their start and end apart: 1, of which 1 were waited for; matrix products, arithmetic and copies ran while one was open for 1% of the time, Pallas kernels for 0%

profile of v5, /device:TPU:1, one launch (start us, length us, event | category | flops | bytes accessed | tf_op | source)
XLA Modules:
  0.0 188.6 jit_solution(6279139470377135336)
XLA Ops:
  0.7 1.2 copy.103
  1.8 1.1 copy.104
  3.0 1.1 copy.105
  4.1 1.1 copy.106
  5.6 1.0 pad_maximum_fusion
  6.6 21.7 %all-to-all-start = ((bf16[64,49,128]{2,1,0:T(8,128)(2,1)}), bf16[64,49,128]{2,1,0:T(8,128)(2,1)S(1)}, u32[]{:S(2)}, u32[]{:S(2)}) async-start(bf16[64,49,128]{2,1,0:T(8,128)(2,1)} %pad_maximum_fusion), calls=%async_computation | async-start | bytes 1835008 | tf_op jit(solution)/shard_map/all_to_all | solution.py:232
  30.9 39.2 %all-to-all-done = bf16[64,49,128]{2,1,0:T(8,128)(2,1)S(1)} async-done(((bf16[64,49,128]{2,1,0:T(8,128)(2,1)}), bf16[64,49,128]{2,1,0:T(8,128)(2,1)S(1)}, u32[]{:S(2)}, u32[]{:S(2)}) %all-to-all-start) | async-done | bytes 802848 | tf_op jit(solution)/shard_map/all_to_all | solution.py:232
  70.9 1.0 fusion.33
  71.9 1.3 convolution_bitcast_fusion
  73.2 0.8 multiply_add_fusion.1
  74.1 2.1 %fusion.12 = f32[32,2,128,128]{2,3,0,1:T(8,128)S(1)} fusion(f32[32,1,128,128]{2,3,1,0:T(8,128)S(1)} %get-tuple-element.38, f32[32,1,128,128]{2,3,1,0:T(8,128)S(1)} %get-tuple-element.37, f32[1,2,128,128]{2,3,0,1:T(8,128)S(1)} %get-tuple-element.64, f32[1,2,128,128]{2,3,0,1:T(8,128)S(1)} %get-tuple-element.71), kind=kOutput, calls=%fused_computation.14 | convolution fusion | flops 1611726848 | bytes 8650752 | tf_op jit(solution)/shard_map/mkab,kjbq->mjaq/dot_general | solution.py:59
  77.3 1.0 multiply_add_fusion.2
  78.6 2.1 %fusion.9 = f32[32,2,128,128]{2,3,1,0:T(8,128)S(1)} fusion(f32[16,2,128,128]{2,3,0,1:T(8,128)S(1)} %maximum_bitcast_fusion.6, f32[16,2,128,128]{2,3,0,1:T(8,128)S(1)} %maximum_bitcast_fusion.5, f32[1,2,128,128]{2,3,1,0:T(8,128)S(1)} %get-tuple-element.72, f32[1,2,128,128]{2,3,1,0:T(8,128)S(1)} %get-tuple-element.63), kind=kOutput, calls=%fused_computation.13 | convolution fusion | flops 1611726848 | bytes 8650752 | tf_op jit(solution)/shard_map/mkab,kjbq->mjaq/dot_general | solution.py:64
  81.6 2.2 %fusion.19 = bf16[64,32,128]{2,0,1:T(8,128)(2,1)S(1)} fusion(f32[32,1,128,128]{2,3,1,0:T(8,128)S(1)} %get-tuple-element.36, f32[32,1,128,128]{2,3,1,0:T(8,128)S(1)} %get-tuple-element.35, f32[1,64,128]{2,1,0:T(8,128)S(1)} %copy-done.7, f32[1,64,128]{2,1,0:T(8,128)S(1)} %copy-done.10), kind=kOutput, calls=%fused_computation.27 | convolution fusion | flops 404242432 | bytes 4784128 | tf_op jit(solution)/shard_map/kna,mkab->nmb/dot_general | solution.py:74
  84.5 1.0 fusion.96
  87.7 1.7 copy.122
  89.3 2.3 %select_reduce_fusion = f32[128]{0:T(128)S(1)} fusion(f32[128,256]{1,0:T(8,128)} %copy.122), kind=kLoop, calls=%fused_computation | loop fusion | flops 16777088 | bytes 131584 | tf_op jit(solution)/shard_map/reduce_sum | solution.py:186
  91.6 1.1 bitcast_convert_fusion
  94.2 0.9 fusion.25
  98.5 20.9 %psum.7 = f32[]{:T(128)} all-reduce(f32[]{:T(128)S(6)} %add.209), channel_id=1, replica_groups=mesh['ctx'=64,'ch'=8] {'ch'}, use_global_device_ids=true, to_apply=%region_4.5 | all-reduce | flops 1 | bytes 8 | tf_op jit(solution)/shard_map/psum | solution.py:189
  121.5 1.7 copy.123
  123.3 57.7 %all_to_all.10 = bf16[64,52,128]{2,1,0:T(8,128)(2,1)S(1)} all-to-all(bf16[64,52,128]{2,1,0:T(8,128)(2,1)S(1)} %copy.123), channel_id=1, replica_groups=mesh['ctx'=64,'ch'=8] {'ctx'}, dimensions={0} | all-to-all | bytes 1703936 | tf_op jit(solution)/shard_map/all_to_all | solution.py:245
  181.3 0.8 copy.126
  183.1 0.8 copy.128
  (96 shorter events, 16.9 us)
Async XLA Ops:
  0.6 27.7 %copy-start = (bf16[128,64]{0,1:T(8,128)(2,1)S(1)}, bf16[128,64]{0,1:T(8,128)(2,1)}, u32[]{:S(2)}) copy-start(bf16[128,64]{0,1:T(8,128)(2,1)} %param.12) | copy-start | bytes 49156
  0.6 4.6 %copy-start.16 = (bf16[128,1024]{1,0:T(8,128)(2,1)S(1)}, bf16[128,1024]{1,0:T(8,128)(2,1)}, u32[]{:S(2)}) copy-start(bf16[128,1024]{1,0:T(8,128)(2,1)} %param.8) | copy-start | bytes 786436
  0.7 4.7 %copy-start.17 = (bf16[128,64]{0,1:T(8,128)(2,1)S(1)}, bf16[128,64]{0,1:T(8,128)(2,1)}, u32[]{:S(2)}) copy-start(bf16[128,64]{0,1:T(8,128)(2,1)} %param.13) | copy-start | bytes 49156
  6.6 63.5 %all-to-all-start = ((bf16[64,49,128]{2,1,0:T(8,128)(2,1)}), bf16[64,49,128]{2,1,0:T(8,128)(2,1)S(1)}, u32[]{:S(2)}, u32[]{:S(2)}) async-start(bf16[64,49,128]{2,1,0:T(8,128)(2,1)} %pad_maximum_fusion), calls=%async_computation | async-start | bytes 1835008 | tf_op jit(solution)/shard_map/all_to_all | solution.py:232
  29.2 41.4 %copy-start.12 = (bf16[1,128,255]{2,1,0:T(8,128)(2,1)}, bf16[1,128,255]{2,1,0:T(8,128)(2,1)S(1)}, u32[]{:S(2)}) copy-start(bf16[1,128,255]{2,1,0:T(8,128)(2,1)S(1)} %reshape.482) | copy-start | bytes 195844
  30.0 46.5 %copy-start.6 = (f32[1,64,128]{2,1,0:T(8,128)}, f32[1,64,128]{2,1,0:T(8,128)S(1)}, u32[]{:S(2)}) copy-start(f32[1,64,128]{2,1,0:T(8,128)S(1)} %get-tuple-element.79) | copy-start | bytes 98308
  30.0 46.5 %copy-start.9 = (f32[1,64,128]{2,1,0:T(8,128)}, f32[1,64,128]{2,1,0:T(8,128)S(1)}, u32[]{:S(2)}) copy-start(f32[1,64,128]{2,1,0:T(8,128)S(1)} %get-tuple-element.80) | copy-start | bytes 98308
  30.9 47.7 %copy-start.3 = (f32[1,2,128,128]{2,3,1,0:T(8,128)}, f32[1,2,128,128]{2,3,1,0:T(8,128)S(1)}, u32[]{:S(2)}) copy-start(f32[1,2,128,128]{2,3,1,0:T(8,128)S(1)} %get-tuple-element.72) | copy-start | bytes 393220
  70.1 0.8 copy-start.14
  80.7 0.9 copy-start.7
  80.7 0.9 copy-start.10
  81.6 2.9 %copy-start.13 = (bf16[1,128,255]{2,1,0:T(8,128)(2,1)S(1)}, bf16[1,128,255]{2,1,0:T(8,128)(2,1)}, u32[]{:S(2)}) copy-start(bf16[1,128,255]{2,1,0:T(8,128)(2,1)} %copy-done.12) | copy-start | bytes 195844
  89.3 3.5 %copy-start.4 = (f32[1,2,128,128]{2,3,1,0:T(8,128)S(1)}, f32[1,2,128,128]{2,3,1,0:T(8,128)}, u32[]{:S(2)}) copy-start(f32[1,2,128,128]{2,3,1,0:T(8,128)} %copy-done.3) | copy-start | bytes 393220
  89.3 4.1 %copy-start.1 = (f32[64,16,128]{2,0,1:T(8,128)S(1)}, f32[64,16,128]{2,0,1:T(8,128)}, u32[]{:S(2)}) copy-start(f32[64,16,128]{2,0,1:T(8,128)} %get-tuple-element.76) | copy-start | bytes 1572868
  89.3 4.9 %copy-start.2 = (f32[128,64,16]{0,1,2:T(8,128)S(1)}, f32[128,64,16]{0,1,2:T(8,128)}, u32[]{:S(2)}) copy-start(f32[128,64,16]{0,1,2:T(8,128)} %fusion.96) | copy-start | bytes 1572868
  89.3 4.9 %copy-start.5 = (bf16[63,1,16,128]{3,0,2,1:T(8,128)(2,1)S(1)}, bf16[63,1,16,128]{3,0,2,1:T(8,128)(2,1)}, u32[]{:S(2)}) copy-start(bf16[63,1,16,128]{3,0,2,1:T(8,128)(2,1)} %slice_bitcast_fusion.2) | copy-start | bytes 774148
  89.3 4.9 %copy-start.15 = (bf16[1,128,127]{2,1,0:T(8,128)(2,1)S(1)}, bf16[1,128,127]{2,1,0:T(8,128)(2,1)}, u32[]{:S(2)}) copy-start(bf16[1,128,127]{2,1,0:T(8,128)(2,1)} %slice.159) | copy-start | bytes 97540
  91.6 5.0 %copy-start.18 = (f32[128]{0:T(128)}, f32[128]{0:T(128)S(1)}, u32[]{:S(2)}) copy-start(f32[128]{0:T(128)S(1)} %select_reduce_fusion) | copy-start | bytes 1540
  92.7 2.4 %copy-start.8 = (f32[1,64,128]{2,1,0:T(8,128)S(1)}, f32[1,64,128]{2,1,0:T(8,128)}, u32[]{:S(2)}) copy-start(f32[1,64,128]{2,1,0:T(8,128)} %copy-done.6) | copy-start | bytes 98308
  92.7 2.4 %copy-start.11 = (f32[1,64,128]{2,1,0:T(8,128)S(1)}, f32[1,64,128]{2,1,0:T(8,128)}, u32[]{:S(2)}) copy-start(f32[1,64,128]{2,1,0:T(8,128)} %copy-done.9) | copy-start | bytes 98308
  92.8 28.0 %copy-start.19 = (bf16[1,128]{1,0:T(2,128)(2,1)S(1)}, bf16[1,128]{1,0:T(2,128)(2,1)}, u32[]{:S(2)}) copy-start(bf16[1,128]{1,0:T(2,128)(2,1)} %get-tuple-element.73) | copy-start | bytes 772

commit v6 on v5

--- a/solution.py
+++ b/solution.py
@@ -176,14 +176,17 @@
     prev_lags = jnp.einsum(
         "ngcs,ngcr->gsr", gated_prev, mixed_items, preferred_element_type=wide_type
     )
-    lag_table = jnp.concatenate([own_lags, prev_lags], axis=2)
-    lag_of = lax.broadcasted_iota(jnp.int32, (tap_count, tap_count, 2 * tap_count), 2) - (
-        lax.broadcasted_iota(jnp.int32, (tap_count, tap_count, 2 * tap_count), 1)
-    )
-    lag_ids = lax.broadcasted_iota(jnp.int32, (tap_count, tap_count, 2 * tap_count), 0)
-    on_lag = lag_of == lag_ids
+    cube = (tap_count, tap_count, tap_count)
+    lag_of = lax.broadcasted_iota(jnp.int32, cube, 2) - lax.broadcasted_iota(jnp.int32, cube, 1)
+    lag_ids = lax.broadcasted_iota(jnp.int32, cube, 0)
+    on_own = (lag_of == lag_ids)[None]
+    on_prev = (lag_of + tap_count == lag_ids)[None]
     grad_medium = (
-        jnp.sum(jnp.where(on_lag[None], lag_table[:, None], 0.0), axis=(2, 3)) * scale
+        jnp.sum(
+            jnp.where(on_own, own_lags[:, None], 0.0) + jnp.where(on_prev, prev_lags[:, None], 0.0),
+            axis=(2, 3),
+        )
+        * scale
     )
     squares = jnp.sum(jnp.square(lagged.astype(wide_type))) + jnp.sum(grad_medium * grad_medium)
     squares = lax.psum(squares, "ch")

time: 189 us -> 179 us (0.947)
  local copies, waits for them, and re-layouts: 16.8 us -> 11 us
  matrix products: 13 us -> 10.1 us
  other arithmetic: 13.6 us -> 11.5 us
    unnamed x56 -> x22, local copies, waits for them, and re-layouts: 9.97 us -> 8.99 us
where the time goes in v6:
time: 179 us
  blocking collectives  78.7 us (44%)
  waiting for transfers between devices  39.9 us (22%)
  starting transfers between devices  21.7 us (12%)
  other arithmetic  11.5 us (6%)
  local copies, waits for them, and re-layouts  11 us (6%)
  matrix products  10.1 us (6%)
  between operations  5.51 us (3%)
    all_to_all x1, blocking collectives, body(): back = lax.all_to_all(returned, 'ctx', 0, 0, tiled=True)  57.7 us
    all_to_all x1, waiting for transfers between devices, body(): arrived = lax.all_to_all(outbound, 'ctx', 0, 0, tiled=True)  39.9 us
    all_to_all x1, starting transfers between devices, body(): arrived = lax.all_to_all(outbound, 'ctx', 0, 0, tiled=True)  21.7 us
    psum x1, blocking collectives, channel_work(): squares = lax.psum(squares, 'ch')  21 us
    unnamed x22, local copies, waits for them, and re-layouts  8.99 us
  transfers between devices with their start and end apart: 1, of which 1 were waited for; matrix products, arithmetic and copies ran while one was open for 1% of the time, Pallas kernels for 0%

profile of v6, /device:TPU:1, one launch (start us, length us, event | category | flops | bytes accessed | tf_op | source)
XLA Modules:
  0.0 178.5 jit_solution(15019823692535973274)
XLA Ops:
  0.7 1.2 copy.100
  1.8 1.1 copy.99
  3.0 1.1 copy.101
  4.1 1.1 copy.102
  5.6 1.0 pad_maximum_fusion
  6.6 21.7 %all-to-all-start = ((bf16[64,49,128]{2,1,0:T(8,128)(2,1)}), bf16[64,49,128]{2,1,0:T(8,128)(2,1)S(1)}, u32[]{:S(2)}, u32[]{:S(2)}) async-start(bf16[64,49,128]{2,1,0:T(8,128)(2,1)} %pad_maximum_fusion), calls=%async_computation | async-start | bytes 1835008 | tf_op jit(solution)/shard_map/all_to_all | solution.py:235
  30.3 39.9 %all-to-all-done = bf16[64,49,128]{2,1,0:T(8,128)(2,1)S(1)} async-done(((bf16[64,49,128]{2,1,0:T(8,128)(2,1)}), bf16[64,49,128]{2,1,0:T(8,128)(2,1)S(1)}, u32[]{:S(2)}, u32[]{:S(2)}) %all-to-all-start) | async-done | bytes 802848 | tf_op jit(solution)/shard_map/all_to_all | solution.py:235
  70.9 1.3 convolution_bitcast_fusion
  72.2 0.8 multiply_add_fusion.1
  73.1 2.1 %fusion.12 = f32[32,2,128,128]{2,3,0,1:T(8,128)S(1)} fusion(f32[32,1,128,128]{2,3,1,0:T(8,128)S(1)} %get-tuple-element.38, f32[32,1,128,128]{2,3,1,0:T(8,128)S(1)} %get-tuple-element.37, f32[1,2,128,128]{2,3,0,1:T(8,128)S(1)} %get-tuple-element.64, f32[1,2,128,128]{2,3,0,1:T(8,128)S(1)} %get-tuple-element.71), kind=kOutput, calls=%fused_computation.16 | convolution fusion | flops 1611726848 | bytes 8650752 | tf_op jit(solution)/shard_map/mkab,kjbq->mjaq/dot_general | solution.py:59
  76.3 1.2 multiply_add_fusion.2
  77.8 2.1 %fusion.9 = f32[32,2,128,128]{2,3,1,0:T(8,128)S(1)} fusion(f32[16,2,128,128]{2,3,0,1:T(8,128)S(1)} %maximum_bitcast_fusion.6, f32[16,2,128,128]{2,3,0,1:T(8,128)S(1)} %maximum_bitcast_fusion.5, f32[1,2,128,128]{2,3,1,0:T(8,128)S(1)} %get-tuple-element.72, f32[1,2,128,128]{2,3,1,0:T(8,128)S(1)} %get-tuple-element.63), kind=kOutput, calls=%fused_computation.15 | convolution fusion | flops 1611726848 | bytes 8650752 | tf_op jit(solution)/shard_map/mkab,kjbq->mjaq/dot_general | solution.py:64
  79.9 0.8 multiply_subtract_fusion
  80.7 2.2 %fusion.19 = bf16[64,32,128]{2,0,1:T(8,128)(2,1)S(1)} fusion(f32[32,1,128,128]{2,3,1,0:T(8,128)S(1)} %get-tuple-element.36, f32[32,1,128,128]{2,3,1,0:T(8,128)S(1)} %get-tuple-element.35, f32[1,64,128]{2,1,0:T(8,128)S(1)} %get-tuple-element.79, f32[1,64,128]{2,1,0:T(8,128)S(1)} %get-tuple-element.80), kind=kOutput, calls=%fused_computation.29 | convolution fusion | flops 404242432 | bytes 4784128 | tf_op jit(solution)/shard_map/kna,mkab->nmb/dot_general | solution.py:74
  83.9 2.5 %add_reduce_fusion = f32[128]{0:T(128)S(1)} fusion(f32[128,128]{1,0:T(8,128)S(1)} %convolution_bitcast_fusion.4, f32[128,128]{1,0:T(8,128)S(1)} %convolution_bitcast_fusion.5), kind=kLoop, calls=%fused_computation | loop fusion | flops 16777088 | bytes 131584 | tf_op jit(solution)/shard_map/reduce_sum | solution.py:185
  88.3 0.6 multiply_reduce_fusion
  90.2 21.0 %psum.7 = f32[]{:T(128)} all-reduce(f32[]{:T(128)S(6)} %add.226), channel_id=1, replica_groups=mesh['ctx'=64,'ch'=8] {'ch'}, use_global_device_ids=true, to_apply=%region_4.5 | all-reduce | flops 1 | bytes 8 | tf_op jit(solution)/shard_map/psum | solution.py:192
  113.2 57.7 %all_to_all.10 = bf16[64,52,128]{2,1,0:T(8,128)(2,1)S(1)} all-to-all(bf16[64,52,128]{2,1,0:T(8,128)(2,1)S(1)} %copy.118), channel_id=1, replica_groups=mesh['ctx'=64,'ch'=8] {'ctx'}, dimensions={0} | all-to-all | bytes 1703936 | tf_op jit(solution)/shard_map/all_to_all | solution.py:248
  171.2 0.8 copy.121
  172.0 0.8 copy.124
  173.0 0.8 copy.123
  173.8 0.8 copy.122
  174.7 0.7 add_reduce_fusion.1
  176.7 0.7 fusion.83
  (60 shorter events, 8.8 us)
Async XLA Ops:
  0.6 27.7 %copy-start = (bf16[128,64]{0,1:T(8,128)(2,1)S(1)}, bf16[128,64]{0,1:T(8,128)(2,1)}, u32[]{:S(2)}) copy-start(bf16[128,64]{0,1:T(8,128)(2,1)} %param.12) | copy-start | bytes 49156
  0.6 4.6 %copy-start.1 = (bf16[128,1024]{1,0:T(8,128)(2,1)S(1)}, bf16[128,1024]{1,0:T(8,128)(2,1)}, u32[]{:S(2)}) copy-start(bf16[128,1024]{1,0:T(8,128)(2,1)} %param.8) | copy-start | bytes 786436
  0.7 4.7 %copy-start.2 = (bf16[128,64]{0,1:T(8,128)(2,1)S(1)}, bf16[128,64]{0,1:T(8,128)(2,1)}, u32[]{:S(2)}) copy-start(bf16[128,64]{0,1:T(8,128)(2,1)} %param.13) | copy-start | bytes 49156
  6.6 63.5 %all-to-all-start = ((bf16[64,49,128]{2,1,0:T(8,128)(2,1)}), bf16[64,49,128]{2,1,0:T(8,128)(2,1)S(1)}, u32[]{:S(2)}, u32[]{:S(2)}) async-start(bf16[64,49,128]{2,1,0:T(8,128)(2,1)} %pad_maximum_fusion), calls=%async_computation | async-start | bytes 1835008 | tf_op jit(solution)/shard_map/all_to_all | solution.py:235

commit v7 on v6

--- a/solution.py
+++ b/solution.py
@@ -110,9 +110,11 @@
 
     gated_items = gated_part.reshape(by_item)
     gated_prev = jnp.concatenate([jnp.zeros_like(gated_items[:1]), gated_items[:-1]], axis=0)
-    mixed = (
-        jnp.einsum("ngcs,gsr->ngcr", gated_items, near, preferred_element_type=wide_type)
-        + jnp.einsum("ngcs,gsr->ngcr", gated_prev, far, preferred_element_type=wide_type)
+    mixed = jnp.einsum(
+        "ngcs,gsr->ngcr",
+        jnp.concatenate([gated_items, gated_prev], axis=3),
+        jnp.concatenate([near, far], axis=1),
+        preferred_element_type=wide_type,
     ).reshape(half_rows, chan_total, radix_cols)
     gate_wide = gate_part.astype(wide_type)
     carried = (gate_wide * mixed).astype(narrow_type)
@@ -165,9 +167,11 @@
     grad_mixed = (grad_carried * gate_wide).astype(narrow_type)
     mixed_items = grad_mixed.reshape(by_item)
     mixed_next = jnp.concatenate([mixed_items[1:], jnp.zeros_like(mixed_items[:1])], axis=0)
-    grad_gated = (
-        jnp.einsum("ngcs,grs->ngcr", mixed_items, near, preferred_element_type=wide_type)
-        + jnp.einsum("ngcs,grs->ngcr", mixed_next, far, preferred_element_type=wide_type)
+    grad_gated = jnp.einsum(
+        "ngcs,grs->ngcr",
+        jnp.concatenate([mixed_items, mixed_next], axis=3),
+        jnp.concatenate([near, far], axis=2),
+        preferred_element_type=wide_type,
     ).reshape(half_rows, chan_total, radix_cols)
     tap_count = filt.shape[0]
     own_lags = jnp.einsum(
@@ -223,13 +227,10 @@
     def token_major(matrix):
         return matrix.T.reshape(ctx_devices, -1, tok_rows)
 
+    streams = jnp.stack([gated_input, grad_inner, second_gate])
+    streams = streams.reshape(3, tok_rows, ctx_devices, chan_share).transpose(2, 0, 3, 1)
     outbound = jnp.concatenate(
-        [
-            token_major(gated_input),
-            token_major(grad_inner),
-            token_major(second_gate),
-            token_major(long_filter),
-        ],
+        [streams.reshape(ctx_devices, 3 * chan_share, tok_rows), token_major(long_filter)],
         axis=1,
     )
     arrived = lax.all_to_all(outbound, "ctx", 0, 0, tiled=True)

time: 179 us -> 179 us (level)
    unnamed x22 -> x23, local copies, waits for them, and re-layouts: 8.99 us -> 9.45 us
where the time goes in v7:
time: 179 us
  blocking collectives  78.7 us (44%)
  waiting for transfers between devices  39.9 us (22%)
  starting transfers between devices  21.7 us (12%)
  local copies, waits for them, and re-layouts  11.7 us (7%)
  other arithmetic  11.6 us (6%)
  matrix products  9.87 us (6%)
  between operations  5.52 us (3%)
    all_to_all x1, blocking collectives, body(): back = lax.all_to_all(returned, 'ctx', 0, 0, tiled=True)  57.7 us
    all_to_all x1, waiting for transfers between devices, body(): arrived = lax.all_to_all(outbound, 'ctx', 0, 0, tiled=True)  39.9 us
    all_to_all x1, starting transfers between devices, body(): arrived = lax.all_to_all(outbound, 'ctx', 0, 0, tiled=True)  21.7 us
    psum x1, blocking collectives, channel_work(): squares = lax.psum(squares, 'ch')  21 us
    unnamed x23, local copies, waits for them, and re-layouts  9.45 us
  transfers between devices with their start and end apart: 1, of which 1 were waited for; matrix products, arithmetic and copies ran while one was open for 1% of the time, Pallas kernels for 0%

profile of v7, /device:TPU:1, one launch (start us, length us, event | category | flops | bytes accessed | tf_op | source)
XLA Modules:
  0.0 179.0 jit_solution(15028085991193708354)
XLA Ops:
  0.7 1.2 copy.101
  1.8 1.1 copy.102
  3.0 1.1 copy.103
  4.1 1.1 copy.104
  6.2 1.0 pad_maximum_fusion
  7.2 21.7 %all-to-all-start = ((bf16[64,49,128]{2,1,0:T(8,128)(2,1)}), bf16[64,49,128]{2,1,0:T(8,128)(2,1)S(1)}, u32[]{:S(2)}, u32[]{:S(2)}) async-start(bf16[64,49,128]{2,1,0:T(8,128)(2,1)} %pad_maximum_fusion), calls=%async_computation | async-start | bytes 1835008 | tf_op jit(solution)/shard_map/all_to_all | solution.py:236
  30.9 39.9 %all-to-all-done = bf16[64,49,128]{2,1,0:T(8,128)(2,1)S(1)} async-done(((bf16[64,49,128]{2,1,0:T(8,128)(2,1)}), bf16[64,49,128]{2,1,0:T(8,128)(2,1)S(1)}, u32[]{:S(2)}, u32[]{:S(2)}) %all-to-all-start) | async-done | bytes 802848 | tf_op jit(solution)/shard_map/all_to_all | solution.py:236
  71.6 1.3 convolution_bitcast_fusion
  72.9 0.8 multiply_add_fusion.1
  73.7 2.1 %fusion.12 = f32[32,2,128,128]{2,3,0,1:T(8,128)S(1)} fusion(f32[32,1,128,128]{2,3,1,0:T(8,128)S(1)} %get-tuple-element.38, f32[32,1,128,128]{2,3,1,0:T(8,128)S(1)} %get-tuple-element.37, f32[1,2,128,128]{2,3,0,1:T(8,128)S(1)} %get-tuple-element.64, f32[1,2,128,128]{2,3,0,1:T(8,128)S(1)} %get-tuple-element.71), kind=kOutput, calls=%fused_computation.16 | convolution fusion | flops 1611726848 | bytes 8650752 | tf_op jit(solution)/shard_map/mkab,kjbq->mjaq/dot_general | solution.py:59
  77.0 1.2 multiply_add_fusion.2
  78.4 2.1 %fusion.9 = f32[32,2,128,128]{2,3,1,0:T(8,128)S(1)} fusion(f32[16,2,128,128]{2,3,0,1:T(8,128)S(1)} %maximum_bitcast_fusion.6, f32[16,2,128,128]{2,3,0,1:T(8,128)S(1)} %maximum_bitcast_fusion.5, f32[1,2,128,128]{2,3,1,0:T(8,128)S(1)} %get-tuple-element.72, f32[1,2,128,128]{2,3,1,0:T(8,128)S(1)} %get-tuple-element.63), kind=kOutput, calls=%fused_computation.15 | convolution fusion | flops 1611726848 | bytes 8650752 | tf_op jit(solution)/shard_map/mkab,kjbq->mjaq/dot_general | solution.py:64
  80.5 0.8 multiply_subtract_fusion
  81.4 2.2 %fusion.19 = bf16[64,32,128]{2,0,1:T(8,128)(2,1)S(1)} fusion(f32[32,1,128,128]{2,3,1,0:T(8,128)S(1)} %get-tuple-element.36, f32[32,1,128,128]{2,3,1,0:T(8,128)S(1)} %get-tuple-element.35, f32[1,64,128]{2,1,0:T(8,128)S(1)} %get-tuple-element.79, f32[1,64,128]{2,1,0:T(8,128)S(1)} %get-tuple-element.80), kind=kOutput, calls=%fused_computation.29 | convolution fusion | flops 404242432 | bytes 4784128 | tf_op jit(solution)/shard_map/kna,mkab->nmb/dot_general | solution.py:74
  84.3 2.5 %add_reduce_fusion = f32[128]{0:T(128)S(1)} fusion(f32[128,128]{1,0:T(8,128)S(1)} %convolution_bitcast_fusion.5, f32[128,128]{1,0:T(8,128)S(1)} %convolution_bitcast_fusion.6), kind=kLoop, calls=%fused_computation | loop fusion | flops 16777088 | bytes 131584 | tf_op jit(solution)/shard_map/reduce_sum | solution.py:189
  88.8 0.6 multiply_reduce_fusion
  90.7 21.0 %psum.7 = f32[]{:T(128)} all-reduce(f32[]{:T(128)S(6)} %add.210), channel_id=1, replica_groups=mesh['ctx'=64,'ch'=8] {'ch'}, use_global_device_ids=true, to_apply=%region_4.5 | all-reduce | flops 1 | bytes 8 | tf_op jit(solution)/shard_map/psum | solution.py:196
  113.6 57.7 %all_to_all.10 = bf16[64,52,128]{2,1,0:T(8,128)(2,1)S(1)} all-to-all(bf16[64,52,128]{2,1,0:T(8,128)(2,1)S(1)} %copy.121), channel_id=1, replica_groups=mesh['ctx'=64,'ch'=8] {'ctx'}, dimensions={0} | all-to-all | bytes 1703936 | tf_op jit(solution)/shard_map/all_to_all | solution.py:249
  171.7 0.8 copy.124
  172.5 0.8 copy.127
  173.5 0.8 copy.126
  174.3 0.8 copy.125
  175.2 0.7 add_reduce_fusion.1
  177.2 0.7 fusion.93
  (63 shorter events, 9.3 us)
Async XLA Ops:
  0.6 28.4 %copy-start = (bf16[128,64]{0,1:T(8,128)(2,1)S(1)}, bf16[128,64]{0,1:T(8,128)(2,1)}, u32[]{:S(2)}) copy-start(bf16[128,64]{0,1:T(8,128)(2,1)} %param.12) | copy-start | bytes 49156
  0.6 4.6 %copy-start.1 = (bf16[128,1024]{1,0:T(8,128)(2,1)S(1)}, bf16[128,1024]{1,0:T(8,128)(2,1)}, u32[]{:S(2)}) copy-start(bf16[128,1024]{1,0:T(8,128)(2,1)} %param.8) | copy-start | bytes 786436
  5.5 0.7 copy-start.2
  7.2 63.5 %all-to-all-start = ((bf16[64,49,128]{2,1,0:T(8,128)(2,1)}), bf16[64,49,128]{2,1,0:T(8,128)(2,1)S(1)}, u32[]{:S(2)}, u32[]{:S(2)}) async-start(bf16[64,49,128]{2,1,0:T(8,128)(2,1)} %pad_maximum_fusion), calls=%async_computation | async-start | bytes 1835008 | tf_op jit(solution)/shard_map/all_to_all | solution.py:236
